TPU v7x, 768 devices: a whole 4x8x12 slice. The times are simulated.
768 devices in a mesh: seq: 24 (over z, core), head: 32 (over x, y).
Axes of the slice: x: 4, y: 8, z: 12, core: 2. Of those that a mesh axis runs over, the one named last changes fastest.
Arguments:
- queries: bfloat16 [32, 12288, 128], P('head', 'seq'), may hold values from -120 to 120
- keys: bfloat16 [32, 12288, 128], P('head', 'seq'), may hold values from -4.5 to 4.5
- values: bfloat16 [32, 12288, 128], P('head', 'seq'), may hold values from -6 to 6
- grad_out: bfloat16 [32, 12288, 128], P('head', 'seq'), may hold values from -6 to 6
- rand_owner: int32 [192, 3], replicated, may hold values from 0 to 23, all different within a row; in each aligned block of 8 rows (0 to 7, 8 to 15, ...) at most 2 rows name the same one
- rand_slot: int32 [192, 3], replicated, may hold values from 0 to 7
- glob_ids: int32 [2], replicated, may hold values from 0 to 7, as said below
Outputs:
- grad_q: bfloat16 [32, 12288, 128], P('head', 'seq')
- grad_k: bfloat16 [32, 12288, 128], P('head', 'seq')
- grad_v: bfloat16 [32, 12288, 128], P('head', 'seq')
Inputs may be any that keep to these rules, and one draw needn't show every extreme that they name: `rand_owner`: in the 8 rows of one device, each row names 3 different seq indices and no index is named more than 2 times; some index is named exactly 2 times. `glob_ids`: 2 different block numbers; the first device's last block is always one of them.
All inputs are finite; a program needn't handle non-finite values.
Results may differ from a plain program's by a relative error of at most 0.022.
Values may be sent and summed in bfloat16 or wider, within the bound.
No kernel may reach another device: no remote copies, remote signals or barrier semaphores. Data moves between devices by JAX's collectives and lax.ppermute only.
A program may use at most 32 MiB of HBM per device.

v0:
```python
import math

import jax
import jax.numpy as jnp
from jax import lax
from jax.sharding import PartitionSpec as P

BLOCK = 64


NEG_FILL = -1e30


def padded(array, sides, width):
    for axis, dim in sides:
        devices, length = (lax.axis_size(axis), array.shape[dim])
        up = [(i, (i + 1) % devices) for i in range(devices - 1)]
        down = [(j, i) for i, j in up]
        last = lax.slice_in_dim(array, length - width, length, axis=dim)
        first = lax.slice_in_dim(array, 0, width, axis=dim)
        before = lax.ppermute(last, axis, up)
        after = lax.ppermute(first, axis, down)
        array = jnp.concatenate([before, array, after], axis=dim)
    return array


def from_root(block, axis, source):
    block = jnp.where(lax.axis_index(axis) == source, block, jnp.zeros_like(block))
    return lax.psum(block, axis)


def block_edges(tensor):
    return padded(tensor, (("seq", 1),), BLOCK)


def local(queries, keys, values, grad_out, rand_owner, rand_slot, glob_ids):
    head_count, row_count, head_width = queries.shape
    block_count = row_count // BLOCK
    rand_count = rand_owner.shape[1]
    glob_count = glob_ids.shape[0]
    seq_count = lax.axis_size("seq")
    seq_place = lax.axis_index("seq")
    slot_count = min(
        block_count, max(2, (2 * block_count * rand_count + seq_count - 1) // seq_count)
    )
    pair_width = 2 * head_width
    score_scale = 1.0 / math.sqrt(head_width)
    paired = jnp.concatenate([keys, values], axis=2)
    paired_blocks = paired.reshape(head_count, block_count, BLOCK, pair_width)
    widened = block_edges(paired).reshape(head_count, block_count + 2, BLOCK, pair_width)
    window_pairs = jnp.stack(
        [widened[:, offset : offset + block_count] for offset in range(3)], axis=2
    )
    global_block = seq_place * block_count + jnp.arange(block_count, dtype=jnp.int32)
    window_ids = global_block[:, None] + jnp.arange(-1, 2, dtype=jnp.int32)[None, :]
    window_ok = (window_ids >= 0) & (window_ids < seq_count * block_count)
    owners_all = rand_owner.reshape(seq_count, block_count * rand_count)
    slots_all = rand_slot.reshape(seq_count, block_count * rand_count)
    owner_hot = (
        owners_all[:, :, None] == jnp.arange(seq_count, dtype=jnp.int32)[None, None, :]
    ).astype(jnp.int32)
    before = jnp.cumsum(owner_hot, axis=1) - owner_hot
    position = jnp.sum(before * owner_hot, axis=2)
    to_here = owners_all == seq_place
    slot_hot = (
        position[:, :, None] == jnp.arange(slot_count, dtype=jnp.int32)[None, None, :]
    ) & to_here[:, :, None]
    send_block = jnp.sum(slot_hot.astype(jnp.int32) * slots_all[:, :, None], axis=1)
    send_used = jnp.any(slot_hot, axis=1)
    my_owner = lax.dynamic_index_in_dim(owners_all, seq_place, 0, keepdims=False)
    my_slot = lax.dynamic_index_in_dim(slots_all, seq_place, 0, keepdims=False)
    my_position = lax.dynamic_index_in_dim(position, seq_place, 0, keepdims=False)
    return_at = my_owner * slot_count + my_position
    wanted = my_owner * block_count + my_slot
    empty_pairs = jnp.zeros((head_count, block_count * rand_count, BLOCK, pair_width), jnp.bfloat16)
    piece_rows = lax.all_gather(paired, "seq", axis=1, tiled=True)
    piece_blocks = piece_rows.shape[1] // BLOCK
    grouped = piece_rows.reshape(head_count, piece_blocks, BLOCK, pair_width)
    inside = (wanted >= 0) & (wanted < piece_blocks)
    taken = jnp.take(grouped, jnp.clip(wanted, 0, piece_blocks - 1), axis=1)
    random_pairs = jnp.where(inside[None, :, None, None], taken, empty_pairs)
    random_pairs = random_pairs.reshape(head_count, block_count, rand_count, BLOCK, pair_width)
    global_local = jnp.take(paired_blocks, glob_ids, axis=1)
    global_pairs = from_root(global_local, "seq", 0)
    global_wide = jnp.broadcast_to(
        global_pairs[:, None], (head_count, block_count, glob_count, BLOCK, pair_width)
    )
    key_pairs = jnp.concatenate([window_pairs, random_pairs, global_wide], axis=2)
    key_part = key_pairs[..., :head_width]
    value_part = key_pairs[..., head_width:]
    key_valid = jnp.concatenate(
        [window_ok, jnp.ones((block_count, rand_count + glob_count), dtype=bool)], axis=1
    )
    query_blocks = queries.reshape(head_count, block_count, BLOCK, head_width)
    cotan_blocks = grad_out.reshape(head_count, block_count, BLOCK, head_width)
    scores = (
        jnp.einsum("hiqd,hiskd->hiqsk", query_blocks, key_part, preferred_element_type=jnp.float32)
        * score_scale
    )
    scores = jnp.where(key_valid[None, :, None, :, None], scores, NEG_FILL)
    row_max = jnp.max(scores, axis=(3, 4), keepdims=True)
    expo_terms = jnp.exp(scores - row_max)
    weights = expo_terms / jnp.sum(expo_terms, axis=(3, 4), keepdims=True)
    weights_low = weights.astype(jnp.bfloat16)
    attended = jnp.einsum(
        "hiqsk,hiskd->hiqd", weights_low, value_part, preferred_element_type=jnp.float32
    )
    delta = jnp.sum(cotan_blocks.astype(jnp.float32) * attended, axis=3)
    grad_values = jnp.einsum(
        "hiqsk,hiqd->hiskd", weights_low, cotan_blocks, preferred_element_type=jnp.float32
    )
    grad_weights = jnp.einsum(
        "hiqd,hiskd->hiqsk", cotan_blocks, value_part, preferred_element_type=jnp.float32
    )
    grad_scores = (weights * (grad_weights - delta[:, :, :, None, None])).astype(jnp.bfloat16)
    grad_query = (
        jnp.einsum("hiqsk,hiskd->hiqd", grad_scores, key_part, preferred_element_type=jnp.float32)
        * score_scale
    )
    grad_keys = (
        jnp.einsum(
            "hiqsk,hiqd->hiskd", grad_scores, query_blocks, preferred_element_type=jnp.float32
        )
        * score_scale
    )
    contrib = jnp.concatenate([grad_keys, grad_values], axis=4)
    wide_grad = jnp.pad(contrib[:, :, 0], ((0, 0), (0, 2), (0, 0), (0, 0)))
    for offset in range(1, 3):
        wide_grad = wide_grad + jnp.pad(
            contrib[:, :, offset], ((0, 0), (offset, 2 - offset), (0, 0), (0, 0))
        )
    edge_out = jnp.concatenate([wide_grad[:, 0], wide_grad[:, block_count + 1]], axis=1).astype(
        jnp.bfloat16
    )
    edge_in = block_edges(edge_out)
    from_left = edge_in[:, :BLOCK].astype(jnp.float32)
    from_right = edge_in[:, 3 * BLOCK :].astype(jnp.float32)
    accum = wide_grad[:, 1 : block_count + 1]
    accum = accum.at[:, 0].add(from_left)
    accum = accum.at[:, block_count - 1].add(from_right)
    random_terms = contrib[:, :, 3 : 3 + rand_count].astype(jnp.bfloat16)
    random_terms = random_terms.reshape(head_count, block_count * rand_count, BLOCK, pair_width)
    outgoing_grads = jnp.zeros(
        (head_count, seq_count * slot_count, BLOCK, pair_width), jnp.bfloat16
    )
    outgoing_grads = outgoing_grads.at[:, return_at].set(random_terms)
    outgoing_grads = outgoing_grads.reshape(head_count, seq_count, slot_count, BLOCK, pair_width)
    returned = lax.all_to_all(outgoing_grads, "seq", split_axis=1, concat_axis=1, tiled=True)
    returned = returned.reshape(head_count, seq_count * slot_count, BLOCK * pair_width)
    block_hot = (
        send_block.reshape(-1)[:, None] == jnp.arange(block_count, dtype=jnp.int32)[None, :]
    ) & send_used.reshape(-1)[:, None]
    gathered = jnp.einsum(
        "cb,ecx->ebx", block_hot.astype(jnp.bfloat16), returned, preferred_element_type=jnp.float32
    )
    accum = accum + gathered.reshape(head_count, block_count, BLOCK, pair_width)
    global_terms = jnp.sum(contrib[:, :, 3 + rand_count :], axis=1)
    global_sums = lax.psum(global_terms.astype(jnp.bfloat16), "seq").astype(jnp.float32)
    at_first = (seq_place == 0).astype(jnp.float32)
    accum = accum.at[:, glob_ids].add(global_sums * at_first)
    grad_q = grad_query.reshape(head_count, row_count, head_width).astype(jnp.bfloat16)
    grad_k = accum[..., :head_width].reshape(head_count, row_count, head_width).astype(jnp.bfloat16)
    grad_v = accum[..., head_width:].reshape(head_count, row_count, head_width).astype(jnp.bfloat16)
    return (grad_q, grad_k, grad_v)


def solution(mesh):
    return jax.shard_map(
        local,
        mesh=mesh,
        in_specs=(
            P("head", "seq", None),
            P("head", "seq", None),
            P("head", "seq", None),
            P("head", "seq", None),
            P(),
            P(),
            P(),
        ),
        out_specs=(P("head", "seq", None), P("head", "seq", None), P("head", "seq", None)),
        check_vma=False,
    )
```

profile of v0, /device:TPU:1, one launch (start us, length us, event | category | flops | bytes accessed | tf_op | source)
XLA Modules:
  0.0 425.4 jit_solution(6914504111656409700)
XLA Ops:
  7.2 1.0 constant_dynamic-update-slice_fusion.1
  8.2 0.9 constant_dynamic-update-slice_fusion
  10.7 5.4 %collective-permute-start = (bf16[1,64,256]{2,1,0:T(8,128)(2,1)S(1)}, bf16[1,64,256]{2,1,0:T(8,128)(2,1)S(1)}, u32[]{:S(2)}, u32[]{:S(2)}) collective-permute-start(bf16[1,64,256]{2,1,0:T(8,128)(2,1)S(1)} %get-tuple-element.38), channel_id=1, source_target_pairs={{0,32},{32,64},{64,96},{96,128},{128,160},{160,192},{192,224},{224... | collective-permute-start | bytes 98312 | tf_op jit(solution)/shard_map/ppermute | solution.py:21
  16.1 8.3 %collective-permute-start.1 = (bf16[1,64,256]{2,1,0:T(8,128)(2,1)S(1)}, bf16[1,64,256]{2,1,0:T(8,128)(2,1)S(1)}, u32[]{:S(2)}, u32[]{:S(2)}) collective-permute-start(bf16[1,64,256]{2,1,0:T(8,128)(2,1)S(1)} %get-tuple-element.39), channel_id=1, source_target_pairs={{32,0},{64,32},{96,64},{128,96},{160,128},{192,160},{224,192},{256... | collective-permute-start | bytes 98312 | tf_op jit(solution)/shard_map/ppermute | solution.py:22
  25.1 1.5 gather_fusion.1
  31.4 1.0 pad_maximum_fusion.1
  32.4 51.0 %all-gather.2.cloned.1.call-done = bf16[1,12288,256]{2,1,0:T(8,128)(2,1)} async-done(((bf16[1,512,256]{2,1,0:T(8,128)(2,1)}), bf16[1,12288,256]{2,1,0:T(8,128)(2,1)}) %all-gather.2.cloned.1.call-update) | async-done | bytes 6291472 | tf_op jit(solution)/shard_map/all_gather | solution.py:76
  83.5 3.4 gather_fusion
  87.2 146.2 %all-reduce.7.cloned.1.call-done = bf16[2,64,256]{2,1,0:T(8,128)(2,1)} async-done(((bf16[2,64,256]{2,1,0:T(8,128)(2,1)}), bf16[2,64,256]{2,1,0:T(8,128)(2,1)}) %all-reduce.7.cloned.1.call-update) | async-done | bytes 65552 | tf_op jit(solution)/shard_map/psum | solution.py:29
  233.4 0.9 broadcast_dynamic-update-slice_fusion
  235.5 1.0 fusion.10
  237.3 0.9 fusion
  239.2 1.4 broadcast.328
  240.5 4.5 %scatter_fusion = bf16[48,64,256]{2,1,0:T(8,128)(2,1)} fusion(bf16[48,64,256]{2,1,0:T(8,128)(2,1)} %broadcast.328, s32[24]{0:T(128)S(1)} %fusion.40, bf16[24,64,256]{2,1,0:T(8,128)(2,1)S(1)} %bitcast.158), kind=kCustom, calls=%fused_computation.2 | custom fusion | bytes 2359392 | tf_op jit(solution)/shard_map/scatter | solution.py:146
  245.1 6.5 %all-to-all-start = ((bf16[1,24,2,64,256]{4,3,2,0,1:T(8,128)(2,1)}), bf16[1,24,2,64,256]{4,3,2,0,1:T(8,128)(2,1)}, u32[]{:S(2)}, u32[]{:S(2)}) async-start(bf16[1,24,2,64,256]{4,3,2,0,1:T(8,128)(2,1)} %bitcast.153), calls=%async_computation | async-start | bytes 3145728 | tf_op jit(solution)/shard_map/all_to_all | solution.py:148
  252.4 1.4 fusion.14
  253.9 3.7 collective-permute-start.2
  257.6 1.1 fusion.9
  259.5 1.9 collective-permute-start.3
  261.5 39.1 %collective-permute-done.2 = bf16[1,64,256]{2,1,0:T(8,128)(2,1)S(1)} collective-permute-done((bf16[1,64,256]{2,1,0:T(8,128)(2,1)S(1)}, bf16[1,64,256]{2,1,0:T(8,128)(2,1)S(1)}, u32[]{:S(2)}, u32[]{:S(2)}) %collective-permute-start.2) | collective-permute-done | bytes 32800 | tf_op jit(solution)/shard_map/ppermute | solution.py:21
  300.5 3.8 collective-permute-done.3
  304.3 109.3 %all-reduce.9.cloned.1.call-done = bf16[1,2,64,256]{3,2,1,0:T(8,128)(2,1)} async-done(((bf16[1,2,64,256]{3,2,1,0:T(8,128)(2,1)}), bf16[1,2,64,256]{3,2,1,0:T(8,128)(2,1)}) %all-reduce.9.cloned.1.call-update) | async-done | bytes 65552 | tf_op jit(solution)/shard_map/psum | solution.py:158
  413.5 0.9 multiply_bitcast_fusion.1
  414.4 2.3 copy.73
  (80 shorter events, 14.0 us)
Async XLA Ops:
  7.2 227.2 %copy-start = (bf16[1,512,128]{2,1,0:T(8,128)(2,1)S(1)}, bf16[1,512,128]{2,1,0:T(8,128)(2,1)}, u32[]{:S(2)}) copy-start(bf16[1,512,128]{2,1,0:T(8,128)(2,1)} %param.11) | copy-start | bytes 393220
  7.2 76.3 %all-gather.2.cloned.1.call-start = ((), (), s32[]{:S(2)}) async-start(), calls=%async_computation.1 | async-start | bytes 6553600 | tf_op jit(solution)/shard_map/all_gather | solution.py:76
  9.1 0.7 copy-start.3
  9.9 223.6 %all-reduce.7.cloned.1.call-start = ((), (), s32[]{:S(2)}) async-start(), calls=%async_computation.2 | async-start | bytes 131072 | tf_op jit(solution)/shard_map/psum | solution.py:29
  10.7 20.7 %collective-permute-start = (bf16[1,64,256]{2,1,0:T(8,128)(2,1)S(1)}, bf16[1,64,256]{2,1,0:T(8,128)(2,1)S(1)}, u32[]{:S(2)}, u32[]{:S(2)}) collective-permute-start(bf16[1,64,256]{2,1,0:T(8,128)(2,1)S(1)} %get-tuple-element.38), channel_id=1, source_target_pairs={{0,32},{32,64},{64,96},{96,128},{128,160},{160,192},{192,224},{224... | collective-permute-start | bytes 98312 | tf_op jit(solution)/shard_map/ppermute | solution.py:21
  16.1 15.3 %collective-permute-start.1 = (bf16[1,64,256]{2,1,0:T(8,128)(2,1)S(1)}, bf16[1,64,256]{2,1,0:T(8,128)(2,1)S(1)}, u32[]{:S(2)}, u32[]{:S(2)}) collective-permute-start(bf16[1,64,256]{2,1,0:T(8,128)(2,1)S(1)} %get-tuple-element.39), channel_id=1, source_target_pairs={{32,0},{64,32},{96,64},{128,96},{160,128},{192,160},{224,192},{256... | collective-permute-start | bytes 98312 | tf_op jit(solution)/shard_map/ppermute | solution.py:22
  234.3 2.9 copy-start.6
  234.3 1.2 copy-start.8
  237.3 1.4 copy-start.1
  238.2 1.0 copy-start.4
  245.1 169.3 %all-to-all-start = ((bf16[1,24,2,64,256]{4,3,2,0,1:T(8,128)(2,1)}), bf16[1,24,2,64,256]{4,3,2,0,1:T(8,128)(2,1)}, u32[]{:S(2)}, u32[]{:S(2)}) async-start(bf16[1,24,2,64,256]{4,3,2,0,1:T(8,128)(2,1)} %bitcast.153), calls=%async_computation | async-start | bytes 3145728 | tf_op jit(solution)/shard_map/all_to_all | solution.py:148
  251.6 162.0 %all-reduce.9.cloned.1.call-start = ((), (), s32[]{:S(2)}) async-start(), calls=%async_computation.3 | async-start | bytes 131072 | tf_op jit(solution)/shard_map/psum | solution.py:158
  252.4 5.2 %copy-start.7 = (bf16[1,8,8,64,256]{4,3,2,1,0:T(8,128)(2,1)S(1)}, bf16[1,8,8,64,256]{4,3,2,1,0:T(8,128)(2,1)}, u32[]{:S(2)}) copy-start(bf16[1,8,8,64,256]{4,3,2,1,0:T(8,128)(2,1)} %copy-done.6) | copy-start | bytes 6291460
  253.7 3.9 copy-start.5
  253.8 5.0 %copy-start.2 = (f32[1,8,8,64,128]{4,3,2,1,0:T(8,128)S(1)}, f32[1,8,8,64,128]{4,3,2,1,0:T(8,128)}, u32[]{:S(2)}) copy-start(f32[1,8,8,64,128]{4,3,2,1,0:T(8,128)} %copy-done.1) | copy-start | bytes 6291460
  253.9 46.6 %collective-permute-start.2 = (bf16[1,64,256]{2,1,0:T(8,128)(2,1)S(1)}, bf16[1,64,256]{2,1,0:T(8,128)(2,1)S(1)}, u32[]{:S(2)}, u32[]{:S(2)}) collective-permute-start(bf16[1,64,256]{2,1,0:T(8,128)(2,1)S(1)} %get-tuple-element.35), channel_id=1, source_target_pairs={{0,32},{32,64},{64,96},{96,128},{128,160},{160,192},{192,224},{224... | collective-permute-start | bytes 98312 | tf_op jit(solution)/shard_map/ppermute | solution.py:21
  259.5 44.8 %collective-permute-start.3 = (bf16[1,64,256]{2,1,0:T(8,128)(2,1)S(1)}, bf16[1,64,256]{2,1,0:T(8,128)(2,1)S(1)}, u32[]{:S(2)}, u32[]{:S(2)}) collective-permute-start(bf16[1,64,256]{2,1,0:T(8,128)(2,1)S(1)} %get-tuple-element.34), channel_id=1, source_target_pairs={{32,0},{64,32},{96,64},{128,96},{160,128},{192,160},{224,192},{256... | collective-permute-start | bytes 98312 | tf_op jit(solution)/shard_map/ppermute | solution.py:22
Sparse Core Ops, SparseCore 0:
  10.4 73.0 all-gather.1
  86.4 146.9 all-reduce.6
  259.6 153.8 all-reduce.8
where the time goes:
time: 427 us; the launch traced here: 425 us
  waiting for transfers between devices  349 us (82%)
  starting transfers between devices  25.9 us (6%)
  local copies, waits for them, and re-layouts  21.3 us (5%)
  between operations  14.2 us (3%)
  other arithmetic  9.53 us (2%)
  matrix products  5.11 us (1%)
    psum x1, waiting for transfers between devices, from_root(): return lax.psum(block, axis)  146 us
    psum x1, waiting for transfers between devices, local(): lax.psum(global_terms.astype(jnp.bfloat16), 'seq').astype(jnp.float32)  109 us
    all_gather x1, waiting for transfers between devices, local(): piece_rows = lax.all_gather(paired, 'seq', axis=1, tiled=True)  51 us
    ppermute x2, waiting for transfers between devices, padded(): before = lax.ppermute(last, axis, up)  39.1 us
    ppermute x2, starting transfers between devices, padded(): after = lax.ppermute(first, axis, down)  10.2 us
    ppermute x2, starting transfers between devices, padded(): before = lax.ppermute(last, axis, up)  9.04 us
  transfers between devices with their start and end apart: 8, of which 5 were waited for; matrix products, arithmetic and copies ran while one was open for 4% of the time, Pallas kernels for 0%

commit v1 on v0

--- a/solution.py
+++ b/solution.py
@@ -80,8 +80,7 @@
     taken = jnp.take(grouped, jnp.clip(wanted, 0, piece_blocks - 1), axis=1)
     random_pairs = jnp.where(inside[None, :, None, None], taken, empty_pairs)
     random_pairs = random_pairs.reshape(head_count, block_count, rand_count, BLOCK, pair_width)
-    global_local = jnp.take(paired_blocks, glob_ids, axis=1)
-    global_pairs = from_root(global_local, "seq", 0)
+    global_pairs = jnp.take(grouped, glob_ids, axis=1)
     global_wide = jnp.broadcast_to(
         global_pairs[:, None], (head_count, block_count, glob_count, BLOCK, pair_width)
     )
@@ -155,7 +154,8 @@
     )
     accum = accum + gathered.reshape(head_count, block_count, BLOCK, pair_width)
     global_terms = jnp.sum(contrib[:, :, 3 + rand_count :], axis=1)
-    global_sums = lax.psum(global_terms.astype(jnp.bfloat16), "seq").astype(jnp.float32)
+    global_parts = lax.all_gather(global_terms.astype(jnp.bfloat16), "seq", axis=0)
+    global_sums = jnp.sum(global_parts.astype(jnp.float32), axis=0)
     at_first = (seq_place == 0).astype(jnp.float32)
     accum = accum.at[:, glob_ids].add(global_sums * at_first)
     grad_q = grad_query.reshape(head_count, row_count, head_width).astype(jnp.bfloat16)

time: 427 us -> 199 us (0.47)
  waiting for transfers between devices: 349 us -> 110 us
  matrix products: 5.11 us -> 10.7 us
    psum x2 -> x0, waiting for transfers between devices: 255 us -> none  [the longest x1 146 us: from_root(): return lax.psum(block, axis)]
    all_gather x0 -> x1, waiting for transfers between devices: none -> 12.8 us  [local(): lax.all_gather(global_terms.astype(jnp.bfloat16), 'seq', axis=0)]
  transfers between devices with their start and end apart: 8 -> 7, of which waited for: 5 -> 4; matrix products, arithmetic and copies ran while one was open for 4% -> 8% of each run, Pallas kernels for 0% -> 0%
where the time goes in v1:
time: 199 us; the launch traced here: 198 us
  waiting for transfers between devices  110 us (55%)
  local copies, waits for them, and re-layouts  25.5 us (13%)
  starting transfers between devices  25.1 us (13%)
  between operations  14.4 us (7%)
  other arithmetic  11.5 us (6%)
  matrix products  10.7 us (5%)
    all_gather x1, waiting for transfers between devices, local(): piece_rows = lax.all_gather(paired, 'seq', axis=1, tiled=True)  51.3 us
    ppermute x2, waiting for transfers between devices, padded(): before = lax.ppermute(last, axis, up)  41.3 us
    all_gather x1, waiting for transfers between devices, local(): lax.all_gather(global_terms.astype(jnp.bfloat16), 'seq', axis=0)  12.8 us
    ppermute x2, starting transfers between devices, padded(): after = lax.ppermute(first, axis, down)  10.2 us
    ppermute x2, starting transfers between devices, padded(): before = lax.ppermute(last, axis, up)  9.04 us
    unnamed x20, local copies, waits for them, and re-layouts  8.3 us
    all_to_all x1, starting transfers between devices, local(): lax.all_to_all(outgoing_grads, 'seq', split_axis=1, concat_axis=1, tiled=...  5.81 us
    ppermute x2, waiting for transfers between devices, padded(): after = lax.ppermute(first, axis, down)  5.01 us
  transfers between devices with their start and end apart: 7, of which 4 were waited for; matrix products, arithmetic and copies ran while one was open for 8% of the time, Pallas kernels for 0%

profile of v1, /device:TPU:1, one launch (start us, length us, event | category | flops | bytes accessed | tf_op | source)
XLA Modules:
  0.0 197.6 jit_solution(3973339621882185745)
XLA Ops:
  7.2 1.0 constant_dynamic-update-slice_fusion.1
  10.6 5.4 %collective-permute-start = (bf16[1,64,256]{2,1,0:T(8,128)(2,1)S(1)}, bf16[1,64,256]{2,1,0:T(8,128)(2,1)S(1)}, u32[]{:S(2)}, u32[]{:S(2)}) collective-permute-start(bf16[1,64,256]{2,1,0:T(8,128)(2,1)S(1)} %get-tuple-element.38), channel_id=1, source_target_pairs={{0,32},{32,64},{64,96},{96,128},{128,160},{160,192},{192,224},{224... | collective-permute-start | bytes 98312 | tf_op jit(solution)/shard_map/ppermute | solution.py:21
  16.0 8.3 %collective-permute-start.1 = (bf16[1,64,256]{2,1,0:T(8,128)(2,1)S(1)}, bf16[1,64,256]{2,1,0:T(8,128)(2,1)S(1)}, u32[]{:S(2)}, u32[]{:S(2)}) collective-permute-start(bf16[1,64,256]{2,1,0:T(8,128)(2,1)S(1)} %get-tuple-element.39), channel_id=1, source_target_pairs={{32,0},{64,32},{96,64},{128,96},{160,128},{192,160},{224,192},{256... | collective-permute-start | bytes 98312 | tf_op jit(solution)/shard_map/ppermute | solution.py:22
  29.1 1.0 pad_maximum_fusion.1
  32.2 51.3 %all-gather.4.cloned.1.call-done = bf16[1,12288,256]{2,1,0:T(8,128)(2,1)} async-done(((bf16[1,512,256]{2,1,0:T(8,128)(2,1)}), bf16[1,12288,256]{2,1,0:T(8,128)(2,1)}) %all-gather.4.cloned.1.call-update) | async-done | bytes 6291472 | tf_op jit(solution)/shard_map/all_gather | solution.py:76
  83.5 3.3 %gather_fusion.1 = bf16[2,64,256]{2,1,0:T(8,128)(2,1)S(1)} fusion(bf16[192,64,256]{2,1,0:T(8,128)(2,1)} %bitcast.152, s32[1024]{0:T(1024)S(1)} %get-tuple-element.44), kind=kCustom, calls=%fused_computation.1 | custom fusion | bytes 131080 | tf_op jit(solution)/shard_map/jit(_take)/gather | solution.py:83
  86.8 3.4 %gather_fusion = bf16[24,64,256]{2,1,0:T(8,128)(2,1)S(1)} fusion(bf16[192,64,256]{2,1,0:T(8,128)(2,1)} %bitcast.153, s32[1024]{0:T(1024)S(1)} %get-tuple-element.45), kind=kCustom, calls=%fused_computation | custom fusion | bytes 1572960 | tf_op jit(solution)/shard_map/jit(_take)/gather | solution.py:80
  90.3 1.3 select_dynamic-update-slice_fusion
  92.4 1.7 bitcast_reduce_fusion
  94.8 2.2 %fusion.10 = f32[8,64]{1,0:T(8,128)S(1)} fusion(bf16[1,8,8,64,256]{4,3,2,1,0:T(8,128)(2,1)} %broadcast_dynamic-update-slice_fusion, bf16[8,64,128]{2,1,0:T(8,128)(2,1)S(1)} %bitcast.154, f32[8,8,64,64]{3,2,1,0:T(8,128)S(1)} %get-tuple-element.43, f32[8,64]{1,0:T(8,128)S(1)} %fusion.3, f32[8,64]{1,0:T(8,128)S(1)} %get-tuple-element.42, ...), kind=kOutput, calls=%fused_computation.32 | convolution fusion | flops 68615680 | bytes 2234432 | tf_op jit(solution)/shard_map/hiqsk,hiskd->hiqd/dot_general | solution.py:104
  97.8 2.9 %fusion = bf16[8,64,8,64]{1,3,2,0:T(8,128)(2,1)S(1)} fusion(bf16[8,64,128,1]{2,1,3,0:T(8,128)(2,1)S(1)} %bitcast.156, f32[8,64]{1,0:T(8,128)S(1)} %fusion.10, bf16[1,8,8,64,256]{4,3,2,1,0:T(8,128)(2,1)} %broadcast_dynamic-update-slice_fusion, f32[8,64]{1,0:T(8,128)S(1)} %fusion.3, f32[8,64]{1,0:T(8,128)S(1)} %get-tuple-element.42, ...), kind=kOutput, calls=%fused_computation.14 | convolution fusion | flops 68943872 | bytes 2758720 | tf_op jit(solution)/shard_map/hiqd,hiskd->hiqsk/dot_general | solution.py:111
  101.7 1.4 broadcast.321
  103.1 4.8 %scatter_fusion = bf16[48,64,256]{2,1,0:T(8,128)(2,1)} fusion(bf16[48,64,256]{2,1,0:T(8,128)(2,1)} %broadcast.321, s32[24]{0:T(128)S(1)} %fusion.38, bf16[24,64,256]{2,1,0:T(8,128)(2,1)S(1)} %bitcast.146), kind=kCustom, calls=%fused_computation.2 | custom fusion | bytes 2359392 | tf_op jit(solution)/shard_map/scatter | solution.py:145
  107.8 5.8 %all-to-all-start = ((bf16[1,24,2,64,256]{4,3,2,0,1:T(8,128)(2,1)}), bf16[1,24,2,64,256]{4,3,2,0,1:T(8,128)(2,1)}, u32[]{:S(2)}, u32[]{:S(2)}) async-start(bf16[1,24,2,64,256]{4,3,2,0,1:T(8,128)(2,1)} %bitcast.141), calls=%async_computation | async-start | bytes 3145728 | tf_op jit(solution)/shard_map/all_to_all | solution.py:147
  113.7 1.7 fusion.11
  116.2 1.2 fusion.14
  117.6 3.7 %collective-permute-start.2 = (bf16[1,64,256]{2,1,0:T(8,128)(2,1)S(1)}, bf16[1,64,256]{2,1,0:T(8,128)(2,1)S(1)}, u32[]{:S(2)}, u32[]{:S(2)}) collective-permute-start(bf16[1,64,256]{2,1,0:T(8,128)(2,1)S(1)} %get-tuple-element.35), channel_id=1, source_target_pairs={{0,32},{32,64},{64,96},{96,128},{128,160},{160,192},{192,224},{224... | collective-permute-start | bytes 98312 | tf_op jit(solution)/shard_map/ppermute | solution.py:21
  121.3 2.4 %fusion.9 = bf16[8,64,128]{2,1,0:T(8,128)(2,1)} fusion(bf16[8,64,8,64]{1,3,2,0:T(8,128)(2,1)S(1)} %copy-done.4, bf16[1,8,8,64,256]{4,3,2,1,0:T(8,128)(2,1)} %broadcast_dynamic-update-slice_fusion), kind=kOutput, calls=%fused_computation.31 | convolution fusion | flops 67239936 | bytes 1703936 | tf_op jit(solution)/shard_map/hiqsk,hiskd->hiqd/dot_general | solution.py:116
  123.7 1.9 collective-permute-start.3
  125.6 41.3 %collective-permute-done.2 = bf16[1,64,256]{2,1,0:T(8,128)(2,1)S(1)} collective-permute-done((bf16[1,64,256]{2,1,0:T(8,128)(2,1)S(1)}, bf16[1,64,256]{2,1,0:T(8,128)(2,1)S(1)}, u32[]{:S(2)}, u32[]{:S(2)}) %collective-permute-start.2) | collective-permute-done | bytes 32800 | tf_op jit(solution)/shard_map/ppermute | solution.py:21
  166.9 5.0 %collective-permute-done.3 = bf16[1,64,256]{2,1,0:T(8,128)(2,1)S(1)} collective-permute-done((bf16[1,64,256]{2,1,0:T(8,128)(2,1)S(1)}, bf16[1,64,256]{2,1,0:T(8,128)(2,1)S(1)}, u32[]{:S(2)}, u32[]{:S(2)}) %collective-permute-start.3) | collective-permute-done | bytes 32800 | tf_op jit(solution)/shard_map/ppermute | solution.py:22
  171.9 12.8 %all-gather.6.cloned.1.call-done = bf16[48,64,256]{2,1,0:T(8,128)(2,1)} async-done(((bf16[2,64,256]{2,1,0:T(8,128)(2,1)}), bf16[48,64,256]{2,1,0:T(8,128)(2,1)}) %all-gather.6.cloned.1.call-update) | async-done | bytes 1572880 | tf_op jit(solution)/shard_map/all_gather | solution.py:157
  184.7 1.7 convert_reduce_fusion
  186.3 2.3 %copy.73 = bf16[6,8,64,256]{3,1,2,0:T(8,128)(2,1)S(1)} copy(bf16[6,8,64,256]{3,2,1,0:T(8,128)(2,1)} %bitcast.61) | data formatting | bytes 3145728
  (71 shorter events, 15.6 us)
Async XLA Ops:
  7.2 85.3 %copy-start = (bf16[1,512,128]{2,1,0:T(8,128)(2,1)S(1)}, bf16[1,512,128]{2,1,0:T(8,128)(2,1)}, u32[]{:S(2)}) copy-start(bf16[1,512,128]{2,1,0:T(8,128)(2,1)} %param.11) | copy-start | bytes 393220
  7.2 76.3 %all-gather.4.cloned.1.call-start = ((), (), s32[]{:S(2)}) async-start(), calls=%async_computation.1 | async-start | bytes 6553600 | tf_op jit(solution)/shard_map/all_gather | solution.py:76
  9.1 0.7 copy-start.2
  10.6 18.4 %collective-permute-start = (bf16[1,64,256]{2,1,0:T(8,128)(2,1)S(1)}, bf16[1,64,256]{2,1,0:T(8,128)(2,1)S(1)}, u32[]{:S(2)}, u32[]{:S(2)}) collective-permute-start(bf16[1,64,256]{2,1,0:T(8,128)(2,1)S(1)} %get-tuple-element.38), channel_id=1, source_target_pairs={{0,32},{32,64},{64,96},{96,128},{128,160},{160,192},{192,224},{224... | collective-permute-start | bytes 98312 | tf_op jit(solution)/shard_map/ppermute | solution.py:21
  16.0 13.1 %collective-permute-start.1 = (bf16[1,64,256]{2,1,0:T(8,128)(2,1)S(1)}, bf16[1,64,256]{2,1,0:T(8,128)(2,1)S(1)}, u32[]{:S(2)}, u32[]{:S(2)}) collective-permute-start(bf16[1,64,256]{2,1,0:T(8,128)(2,1)S(1)} %get-tuple-element.39), channel_id=1, source_target_pairs={{32,0},{64,32},{96,64},{128,96},{160,128},{192,160},{224,192},{256... | collective-permute-start | bytes 98312 | tf_op jit(solution)/shard_map/ppermute | solution.py:22
  92.4 2.4 %copy-start.5 = (bf16[1,512,128]{2,1,0:T(8,128)(2,1)S(1)}, bf16[1,512,128]{2,1,0:T(8,128)(2,1)}, u32[]{:S(2)}) copy-start(bf16[1,512,128]{2,1,0:T(8,128)(2,1)} %param.14) | copy-start | bytes 393220
  97.8 3.3 %copy-start.1 = (f32[1,8,8,64,128]{4,3,2,1,0:T(8,128)}, f32[1,8,8,64,128]{4,3,2,1,0:T(8,128)S(1)}, u32[]{:S(2)}) copy-start(f32[1,8,8,64,128]{4,3,2,1,0:T(8,128)S(1)} %convolution_bitcast_fusion) | copy-start | bytes 6291460
  100.6 1.0 copy-start.3
  107.8 78.5 %all-to-all-start = ((bf16[1,24,2,64,256]{4,3,2,0,1:T(8,128)(2,1)}), bf16[1,24,2,64,256]{4,3,2,0,1:T(8,128)(2,1)}, u32[]{:S(2)}, u32[]{:S(2)}) async-start(bf16[1,24,2,64,256]{4,3,2,0,1:T(8,128)(2,1)} %bitcast.141), calls=%async_computation | async-start | bytes 3145728 | tf_op jit(solution)/shard_map/all_to_all | solution.py:147
  113.7 71.0 %all-gather.6.cloned.1.call-start = ((), (), s32[]{:S(2)}) async-start(), calls=%async_computation.2 | async-start | bytes 1638400 | tf_op jit(solution)/shard_map/all_gather | solution.py:157
  117.4 3.8 %copy-start.4 = (bf16[8,64,8,64]{1,3,2,0:T(8,128)(2,1)S(1)}, bf16[8,64,8,64]{1,3,2,0:T(8,128)(2,1)}, u32[]{:S(2)}) copy-start(bf16[8,64,8,64]{1,3,2,0:T(8,128)(2,1)} %copy-done.3) | copy-start | bytes 1572868
  117.6 49.3 %collective-permute-start.2 = (bf16[1,64,256]{2,1,0:T(8,128)(2,1)S(1)}, bf16[1,64,256]{2,1,0:T(8,128)(2,1)S(1)}, u32[]{:S(2)}, u32[]{:S(2)}) collective-permute-start(bf16[1,64,256]{2,1,0:T(8,128)(2,1)S(1)} %get-tuple-element.35), channel_id=1, source_target_pairs={{0,32},{32,64},{64,96},{96,128},{128,160},{160,192},{192,224},{224... | collective-permute-start | bytes 98312 | tf_op jit(solution)/shard_map/ppermute | solution.py:21
  123.7 48.2 %collective-permute-start.3 = (bf16[1,64,256]{2,1,0:T(8,128)(2,1)S(1)}, bf16[1,64,256]{2,1,0:T(8,128)(2,1)S(1)}, u32[]{:S(2)}, u32[]{:S(2)}) collective-permute-start(bf16[1,64,256]{2,1,0:T(8,128)(2,1)S(1)} %get-tuple-element.34), channel_id=1, source_target_pairs={{32,0},{64,32},{96,64},{128,96},{160,128},{192,160},{224,192},{256... | collective-permute-start | bytes 98312 | tf_op jit(solution)/shard_map/ppermute | solution.py:22
Sparse Core Ops, SparseCore 0:
  10.4 73.0 all-gather.3
  117.5 67.1 all-gather.5

commit v2 on v1

--- a/solution.py
+++ b/solution.py
@@ -9,28 +9,6 @@
 
 
 NEG_FILL = -1e30
-
-
-def padded(array, sides, width):
-    for axis, dim in sides:
-        devices, length = (lax.axis_size(axis), array.shape[dim])
-        up = [(i, (i + 1) % devices) for i in range(devices - 1)]
-        down = [(j, i) for i, j in up]
-        last = lax.slice_in_dim(array, length - width, length, axis=dim)
-        first = lax.slice_in_dim(array, 0, width, axis=dim)
-        before = lax.ppermute(last, axis, up)
-        after = lax.ppermute(first, axis, down)
-        array = jnp.concatenate([before, array, after], axis=dim)
-    return array
-
-
-def from_root(block, axis, source):
-    block = jnp.where(lax.axis_index(axis) == source, block, jnp.zeros_like(block))
-    return lax.psum(block, axis)
-
-
-def block_edges(tensor):
-    return padded(tensor, (("seq", 1),), BLOCK)
 
 
 def local(queries, keys, values, grad_out, rand_owner, rand_slot, glob_ids):
@@ -47,7 +25,12 @@
     score_scale = 1.0 / math.sqrt(head_width)
     paired = jnp.concatenate([keys, values], axis=2)
     paired_blocks = paired.reshape(head_count, block_count, BLOCK, pair_width)
-    widened = block_edges(paired).reshape(head_count, block_count + 2, BLOCK, pair_width)
+    piece_rows = lax.all_gather(paired, "seq", axis=1, tiled=True)
+    row_start = seq_place * row_count
+    edge_before = lax.dynamic_slice_in_dim(piece_rows, row_start - BLOCK, BLOCK, axis=1)
+    edge_after = lax.dynamic_slice_in_dim(piece_rows, row_start + row_count, BLOCK, axis=1)
+    widened = jnp.concatenate([edge_before, paired, edge_after], axis=1)
+    widened = widened.reshape(head_count, block_count + 2, BLOCK, pair_width)
     window_pairs = jnp.stack(
         [widened[:, offset : offset + block_count] for offset in range(3)], axis=2
     )
@@ -73,7 +56,6 @@
     return_at = my_owner * slot_count + my_position
     wanted = my_owner * block_count + my_slot
     empty_pairs = jnp.zeros((head_count, block_count * rand_count, BLOCK, pair_width), jnp.bfloat16)
-    piece_rows = lax.all_gather(paired, "seq", axis=1, tiled=True)
     piece_blocks = piece_rows.shape[1] // BLOCK
     grouped = piece_rows.reshape(head_count, piece_blocks, BLOCK, pair_width)
     inside = (wanted >= 0) & (wanted < piece_blocks)
@@ -131,9 +113,16 @@
     edge_out = jnp.concatenate([wide_grad[:, 0], wide_grad[:, block_count + 1]], axis=1).astype(
         jnp.bfloat16
     )
-    edge_in = block_edges(edge_out)
-    from_left = edge_in[:, :BLOCK].astype(jnp.float32)
-    from_right = edge_in[:, 3 * BLOCK :].astype(jnp.float32)
+    edge_out = edge_out.reshape(head_count, 2, BLOCK, pair_width)
+    global_terms = jnp.sum(contrib[:, :, 3 + rand_count :], axis=1).astype(jnp.bfloat16)
+    shared_out = jnp.concatenate([edge_out, global_terms], axis=1)
+    shared_in = lax.all_gather(shared_out, "seq", axis=0)
+    left_in = lax.dynamic_index_in_dim(shared_in, jnp.maximum(seq_place - 1, 0), 0, keepdims=False)
+    right_in = lax.dynamic_index_in_dim(
+        shared_in, jnp.minimum(seq_place + 1, seq_count - 1), 0, keepdims=False
+    )
+    from_left = jnp.where(seq_place > 0, left_in[:, 1].astype(jnp.float32), 0.0)
+    from_right = jnp.where(seq_place < seq_count - 1, right_in[:, 0].astype(jnp.float32), 0.0)
     accum = wide_grad[:, 1 : block_count + 1]
     accum = accum.at[:, 0].add(from_left)
     accum = accum.at[:, block_count - 1].add(from_right)
@@ -153,9 +142,7 @@
         "cb,ecx->ebx", block_hot.astype(jnp.bfloat16), returned, preferred_element_type=jnp.float32
     )
     accum = accum + gathered.reshape(head_count, block_count, BLOCK, pair_width)
-    global_terms = jnp.sum(contrib[:, :, 3 + rand_count :], axis=1)
-    global_parts = lax.all_gather(global_terms.astype(jnp.bfloat16), "seq", axis=0)
-    global_sums = jnp.sum(global_parts.astype(jnp.float32), axis=0)
+    global_sums = jnp.sum(shared_in[:, :, 2:].astype(jnp.float32), axis=0)
     at_first = (seq_place == 0).astype(jnp.float32)
     accum = accum.at[:, glob_ids].add(global_sums * at_first)
     grad_q = grad_query.reshape(head_count, row_count, head_width).astype(jnp.bfloat16)

time: 199 us -> 197 us (0.990)
  waiting for transfers between devices: 110 us -> 137 us
  starting transfers between devices: 25.1 us -> 6.02 us
  local copies, waits for them, and re-layouts: 25.5 us -> 21.1 us
  matrix products: 10.7 us -> 6.64 us
    all_to_all x1, waiting for transfers between devices: 0.01 us -> 66.8 us  [local(): lax.all_to_all(outgoing_grads, 'seq', split_axis=1, concat_axis=1, tiled=...]
    ppermute x4 -> x0, waiting for transfers between devices: 46.3 us -> none  [the longest x2 41.3 us: padded(): before = lax.ppermute(last, axis, up)]
    ppermute x4 -> x0, starting transfers between devices: 19.2 us -> none  [the longest x2 10.2 us: padded(): after = lax.ppermute(first, axis, down)]
    all_gather x1, waiting for transfers between devices: 51.3 us -> 68.8 us  [local(): piece_rows = lax.all_gather(paired, 'seq', axis=1, tiled=True)]
    all_gather x1, waiting for transfers between devices: 12.8 us -> 1.39 us  [local(): shared_in = lax.all_gather(shared_out, 'seq', axis=0)]
    unnamed x20 -> x24, local copies, waits for them, and re-layouts: 8.3 us -> 4.82 us
    another operation x3, other arithmetic: 0.29 us -> 2.31 us
  transfers between devices with their start and end apart: 7 -> 3, of which waited for: 4 -> 3; matrix products, arithmetic and copies ran while one was open for 8% -> 9% of each run, Pallas kernels for 0% -> 0%
where the time goes in v2:
time: 197 us; the launch traced here: 196 us
  waiting for transfers between devices  137 us (70%)
  local copies, waits for them, and re-layouts  21.1 us (11%)
  between operations  14.4 us (7%)
  other arithmetic  11.1 us (6%)
  matrix products  6.64 us (3%)
  starting transfers between devices  6.02 us (3%)
    all_gather x1, waiting for transfers between devices, local(): piece_rows = lax.all_gather(paired, 'seq', axis=1, tiled=True)  68.8 us
    all_to_all x1, waiting for transfers between devices, local(): lax.all_to_all(outgoing_grads, 'seq', split_axis=1, concat_axis=1, tiled=...  66.8 us
    all_to_all x1, starting transfers between devices, local(): lax.all_to_all(outgoing_grads, 'seq', split_axis=1, concat_axis=1, tiled=...  5.94 us
    unnamed x24, local copies, waits for them, and re-layouts  4.82 us
    scatter x1, local copies, waits for them, and re-layouts, local(): outgoing_grads = outgoing_grads.at[:, return_at].set(random_terms)  4.66 us
  transfers between devices with their start and end apart: 3, of which 3 were waited for; matrix products, arithmetic and copies ran while one was open for 9% of the time, Pallas kernels for 0%

profile of v2, /device:TPU:1, one launch (start us, length us, event | category | flops | bytes accessed | tf_op | source)
XLA Modules:
  0.0 196.3 jit_solution(4229908835866887116)
XLA Ops:
  7.2 1.0 constant_dynamic-update-slice_fusion.1
  8.2 0.9 constant_dynamic-update-slice_fusion
  9.9 0.8 copy.50
  10.9 0.8 copy.52
  12.2 0.7 fusion.43
  14.7 68.8 %all-gather.4.cloned.1.call-done = bf16[1,12288,256]{2,1,0:T(8,128)(2,1)} async-done(((bf16[1,512,256]{2,1,0:T(8,128)(2,1)}), bf16[1,12288,256]{2,1,0:T(8,128)(2,1)}) %all-gather.4.cloned.1.call-update) | async-done | bytes 6291472 | tf_op jit(solution)/shard_map/all_gather | solution.py:28
  83.5 3.3 %gather_fusion.1 = bf16[2,64,256]{2,1,0:T(8,128)(2,1)S(1)} fusion(bf16[192,64,256]{2,1,0:T(8,128)(2,1)} %bitcast.149, s32[1024]{0:T(1024)S(1)} %get-tuple-element.44), kind=kCustom, calls=%fused_computation.1 | custom fusion | bytes 131080 | tf_op jit(solution)/shard_map/jit(_take)/gather | solution.py:65
  86.8 3.4 %gather_fusion = bf16[24,64,256]{2,1,0:T(8,128)(2,1)S(1)} fusion(bf16[192,64,256]{2,1,0:T(8,128)(2,1)} %bitcast.150, s32[1024]{0:T(1024)S(1)} %get-tuple-element.45), kind=kCustom, calls=%fused_computation | custom fusion | bytes 1572960 | tf_op jit(solution)/shard_map/jit(_take)/gather | solution.py:62
  90.2 0.8 constant_dynamic-slice_fusion.2
  92.8 1.0 fusion.9
  94.5 0.9 fusion
  96.6 1.1 fusion.41
  98.3 1.2 fusion.4
  99.6 1.4 broadcast.341
  101.0 4.7 %scatter_fusion = bf16[48,64,256]{2,1,0:T(8,128)(2,1)} fusion(bf16[48,64,256]{2,1,0:T(8,128)(2,1)} %broadcast.341, s32[24]{0:T(128)S(1)} %fusion.38, bf16[24,64,256]{2,1,0:T(8,128)(2,1)S(1)} %bitcast.143), kind=kCustom, calls=%fused_computation.2 | custom fusion | bytes 2359392 | tf_op jit(solution)/shard_map/scatter | solution.py:134
  105.6 5.9 %all-to-all-start = ((bf16[1,24,2,64,256]{4,3,2,0,1:T(8,128)(2,1)}), bf16[1,24,2,64,256]{4,3,2,0,1:T(8,128)(2,1)S(1)}, u32[]{:S(2)}, u32[]{:S(2)}) async-start(bf16[1,24,2,64,256]{4,3,2,0,1:T(8,128)(2,1)} %bitcast.39), calls=%async_computation | async-start | bytes 3145728 | tf_op jit(solution)/shard_map/all_to_all | solution.py:136
  112.4 2.7 %fusion.8 = bf16[8,64,128]{2,1,0:T(8,128)(2,1)} fusion(bf16[8,64,8,64]{1,3,2,0:T(8,128)(2,1)} %copy-done.5, bf16[1,8,8,64,256]{4,3,2,1,0:T(8,128)(2,1)} %copy-done.6), kind=kOutput, calls=%fused_computation.31 | convolution fusion | flops 67239936 | bytes 2228224 | tf_op jit(solution)/shard_map/hiqsk,hiskd->hiqd/dot_general | solution.py:98
  115.0 66.8 %all-to-all-done = bf16[1,24,2,64,256]{4,3,2,0,1:T(8,128)(2,1)S(1)} async-done(((bf16[1,24,2,64,256]{4,3,2,0,1:T(8,128)(2,1)}), bf16[1,24,2,64,256]{4,3,2,0,1:T(8,128)(2,1)S(1)}, u32[]{:S(2)}, u32[]{:S(2)}) %all-to-all-start) | async-done | bytes 1572896 | tf_op jit(solution)/shard_map/all_to_all | solution.py:136
  181.8 0.9 copy.73
  183.2 1.4 all-gather.6.cloned.1.call-done
  184.6 1.6 convert_reduce_fusion
  186.2 0.8 fusion.28
  187.0 0.8 fusion.27
  188.7 0.8 fusion.42
  (69 shorter events, 9.4 us)
Async XLA Ops:
  7.2 84.5 %copy-start = (bf16[1,512,128]{2,1,0:T(8,128)(2,1)S(1)}, bf16[1,512,128]{2,1,0:T(8,128)(2,1)}, u32[]{:S(2)}) copy-start(bf16[1,512,128]{2,1,0:T(8,128)(2,1)} %param.11) | copy-start | bytes 393220
  7.2 76.3 %all-gather.4.cloned.1.call-start = ((), (), s32[]{:S(2)}) async-start(), calls=%async_computation.1 | async-start | bytes 6553600 | tf_op jit(solution)/shard_map/all_gather | solution.py:28
  9.1 0.7 copy-start.3
  9.9 81.2 %copy-start.4 = (bf16[1,512,256]{2,1,0:T(8,128)(2,1)S(1)}, bf16[1,512,256]{2,1,0:T(8,128)(2,1)}, u32[]{:S(2)}) copy-start(bf16[1,512,256]{2,1,0:T(8,128)(2,1)} %copy-done.3) | copy-start | bytes 786436
  9.9 174.7 %all-gather.6.cloned.1.call-start = ((), (), s32[]{:S(2)}) async-start(), calls=%async_computation.2 | async-start | bytes 3276800 | tf_op jit(solution)/shard_map/all_gather | solution.py:119
  91.6 2.9 %copy-start.6 = (bf16[1,8,8,64,256]{4,3,2,1,0:T(8,128)(2,1)}, bf16[1,8,8,64,256]{4,3,2,1,0:T(8,128)(2,1)S(1)}, u32[]{:S(2)}) copy-start(bf16[1,8,8,64,256]{4,3,2,1,0:T(8,128)(2,1)S(1)} %broadcast_dynamic-update-slice_fusion) | copy-start | bytes 6291460
  91.6 1.2 copy-start.7
  94.5 1.4 copy-start.1
  95.4 1.0 copy-start.5
  105.6 6.7 %copy-start.2 = (f32[1,10,64,256]{3,2,1,0:T(8,128)S(1)}, f32[1,10,64,256]{3,2,1,0:T(8,128)}, u32[]{:S(2)}) copy-start(f32[1,10,64,256]{3,2,1,0:T(8,128)} %get-tuple-element.30) | copy-start | bytes 1966084
  105.6 76.2 %all-to-all-start = ((bf16[1,24,2,64,256]{4,3,2,0,1:T(8,128)(2,1)}), bf16[1,24,2,64,256]{4,3,2,0,1:T(8,128)(2,1)S(1)}, u32[]{:S(2)}, u32[]{:S(2)}) async-start(bf16[1,24,2,64,256]{4,3,2,0,1:T(8,128)(2,1)} %bitcast.39), calls=%async_computation | async-start | bytes 3145728 | tf_op jit(solution)/shard_map/all_to_all | solution.py:136
Sparse Core Ops, SparseCore 0:
  10.4 73.0 all-gather.3
  98.4 86.0 all-gather.5

commit v3 on v2

--- a/solution.py
+++ b/solution.py
@@ -55,14 +55,18 @@
     my_position = lax.dynamic_index_in_dim(position, seq_place, 0, keepdims=False)
     return_at = my_owner * slot_count + my_position
     wanted = my_owner * block_count + my_slot
-    empty_pairs = jnp.zeros((head_count, block_count * rand_count, BLOCK, pair_width), jnp.bfloat16)
     piece_blocks = piece_rows.shape[1] // BLOCK
-    grouped = piece_rows.reshape(head_count, piece_blocks, BLOCK, pair_width)
-    inside = (wanted >= 0) & (wanted < piece_blocks)
-    taken = jnp.take(grouped, jnp.clip(wanted, 0, piece_blocks - 1), axis=1)
-    random_pairs = jnp.where(inside[None, :, None, None], taken, empty_pairs)
-    random_pairs = random_pairs.reshape(head_count, block_count, rand_count, BLOCK, pair_width)
-    global_pairs = jnp.take(grouped, glob_ids, axis=1)
+    grouped = piece_rows.reshape(head_count, piece_blocks, BLOCK * pair_width)
+    pick_ids = jnp.concatenate([wanted, glob_ids.astype(jnp.int32)])
+    pick_hot = pick_ids[:, None] == jnp.arange(piece_blocks, dtype=jnp.int32)[None, :]
+    picked = jnp.einsum(
+        "pc,hcx->hpx", pick_hot.astype(jnp.bfloat16), grouped, preferred_element_type=jnp.float32
+    ).astype(jnp.bfloat16)
+    picked = picked.reshape(head_count, block_count * rand_count + glob_count, BLOCK, pair_width)
+    random_pairs = picked[:, : block_count * rand_count].reshape(
+        head_count, block_count, rand_count, BLOCK, pair_width
+    )
+    global_pairs = picked[:, block_count * rand_count :]
     global_wide = jnp.broadcast_to(
         global_pairs[:, None], (head_count, block_count, glob_count, BLOCK, pair_width)
     )
@@ -98,23 +102,42 @@
         jnp.einsum("hiqsk,hiskd->hiqd", grad_scores, key_part, preferred_element_type=jnp.float32)
         * score_scale
     )
-    grad_keys = (
-        jnp.einsum(
-            "hiqsk,hiqd->hiskd", grad_scores, query_blocks, preferred_element_type=jnp.float32
+    def key_terms(first, last):
+        keys_now = jnp.einsum(
+            "hiqsk,hiqd->hiskd",
+            grad_scores[:, :, :, first:last],
+            query_blocks,
+            preferred_element_type=jnp.float32,
         )
-        * score_scale
-    )
-    contrib = jnp.concatenate([grad_keys, grad_values], axis=4)
-    wide_grad = jnp.pad(contrib[:, :, 0], ((0, 0), (0, 2), (0, 0), (0, 0)))
+        values_now = jnp.einsum(
+            "hiqsk,hiqd->hiskd",
+            weights_low[:, :, :, first:last],
+            cotan_blocks,
+            preferred_element_type=jnp.float32,
+        )
+        return jnp.concatenate([keys_now * score_scale, values_now], axis=4)
+
+    random_terms = key_terms(3, 3 + rand_count).astype(jnp.bfloat16)
+    random_terms = random_terms.reshape(head_count, block_count * rand_count, BLOCK * pair_width)
+    slot_ids = jnp.arange(seq_count * slot_count, dtype=jnp.int32)
+    send_hot = slot_ids[:, None] == return_at[None, :]
+    outgoing_grads = jnp.einsum(
+        "ti,hix->htx", send_hot.astype(jnp.bfloat16), random_terms, preferred_element_type=jnp.float32
+    ).astype(jnp.bfloat16)
+    outgoing_grads = outgoing_grads.reshape(head_count, seq_count, slot_count, BLOCK, pair_width)
+    returned = lax.all_to_all(outgoing_grads, "seq", split_axis=1, concat_axis=1, tiled=True)
+    window_terms = key_terms(0, 3)
+    global_full = key_terms(3 + rand_count, 3 + rand_count + glob_count)
+    wide_grad = jnp.pad(window_terms[:, :, 0], ((0, 0), (0, 2), (0, 0), (0, 0)))
     for offset in range(1, 3):
         wide_grad = wide_grad + jnp.pad(
-            contrib[:, :, offset], ((0, 0), (offset, 2 - offset), (0, 0), (0, 0))
+            window_terms[:, :, offset], ((0, 0), (offset, 2 - offset), (0, 0), (0, 0))
         )
     edge_out = jnp.concatenate([wide_grad[:, 0], wide_grad[:, block_count + 1]], axis=1).astype(
         jnp.bfloat16
     )
     edge_out = edge_out.reshape(head_count, 2, BLOCK, pair_width)
-    global_terms = jnp.sum(contrib[:, :, 3 + rand_count :], axis=1).astype(jnp.bfloat16)
+    global_terms = jnp.sum(global_full, axis=1).astype(jnp.bfloat16)
     shared_out = jnp.concatenate([edge_out, global_terms], axis=1)
     shared_in = lax.all_gather(shared_out, "seq", axis=0)
     left_in = lax.dynamic_index_in_dim(shared_in, jnp.maximum(seq_place - 1, 0), 0, keepdims=False)
@@ -126,14 +149,6 @@
     accum = wide_grad[:, 1 : block_count + 1]
     accum = accum.at[:, 0].add(from_left)
     accum = accum.at[:, block_count - 1].add(from_right)
-    random_terms = contrib[:, :, 3 : 3 + rand_count].astype(jnp.bfloat16)
-    random_terms = random_terms.reshape(head_count, block_count * rand_count, BLOCK, pair_width)
-    outgoing_grads = jnp.zeros(
-        (head_count, seq_count * slot_count, BLOCK, pair_width), jnp.bfloat16
-    )
-    outgoing_grads = outgoing_grads.at[:, return_at].set(random_terms)
-    outgoing_grads = outgoing_grads.reshape(head_count, seq_count, slot_count, BLOCK, pair_width)
-    returned = lax.all_to_all(outgoing_grads, "seq", split_axis=1, concat_axis=1, tiled=True)
     returned = returned.reshape(head_count, seq_count * slot_count, BLOCK * pair_width)
     block_hot = (
         send_block.reshape(-1)[:, None] == jnp.arange(block_count, dtype=jnp.int32)[None, :]

time: 197 us -> 201 us (1.020)
  matrix products: 6.64 us -> 11.5 us
  other arithmetic: 11.1 us -> 8.36 us
    another operation x0 -> x1, local copies, waits for them, and re-layouts: none -> 10.5 us
    gather x2 -> x0, local copies, waits for them, and re-layouts: 6.71 us -> none  [the longest x1 3.38 us: local(): taken = jnp.take(grouped, jnp.clip(wanted, 0, piece_blocks - 1), axis=1)]
    dot_general x2 -> x8, matrix products: 1.09 us -> 5.96 us  [the longest x1 4.07 us: local(): jnp.einsum('pc,hcx->hpx', pick_hot.astype(jnp.bfloat16), grouped, preferr...]
    scatter x1 -> x0, local copies, waits for them, and re-layouts: 4.66 us -> none  [local(): outgoing_grads = outgoing_grads.at[:, return_at].set(random_terms)]
    unnamed x24 -> x26, local copies, waits for them, and re-layouts: 4.82 us -> 7 us
    another operation x3 -> x2, other arithmetic: 2.31 us -> 0.17 us
  transfers between devices with their start and end apart: 3 -> 3, of which waited for: 3 -> 3; matrix products, arithmetic and copies ran while one was open for 9% -> 6% of each run, Pallas kernels for 0% -> 0%
where the time goes in v3:
time: 201 us
  waiting for transfers between devices  139 us (69%)
  local copies, waits for them, and re-layouts  20.9 us (10%)
  between operations  14.5 us (7%)
  matrix products  11.5 us (6%)
  other arithmetic  8.36 us (4%)
  starting transfers between devices  6.05 us (3%)
    all_gather x1, waiting for transfers between devices, local(): piece_rows = lax.all_gather(paired, 'seq', axis=1, tiled=True)  69.8 us
    all_to_all x1, waiting for transfers between devices, local(): lax.all_to_all(outgoing_grads, 'seq', split_axis=1, concat_axis=1, tiled=...  66.8 us
    another operation x1, local copies, waits for them, and re-layouts  10.5 us
    unnamed x26, local copies, waits for them, and re-layouts  7 us
    all_to_all x1, starting transfers between devices, local(): lax.all_to_all(outgoing_grads, 'seq', split_axis=1, concat_axis=1, tiled=...  5.97 us
    dot_general x1, matrix products, local(): jnp.einsum('pc,hcx->hpx', pick_hot.astype(jnp.bfloat16), grouped, preferr...  4.07 us
  transfers between devices with their start and end apart: 3, of which 3 were waited for; matrix products, arithmetic and copies ran while one was open for 6% of the time, Pallas kernels for 0%

profile of v3, /device:TPU:1, one launch (start us, length us, event | category | flops | bytes accessed | tf_op | source)
XLA Modules:
  0.0 200.6 jit_solution(13557591871079182629)
XLA Ops:
  7.2 1.0 constant_dynamic-update-slice_fusion.1
  8.2 0.9 constant_dynamic-update-slice_fusion
  9.1 0.7 copy-done.1
  9.9 0.8 copy.52
  10.9 0.8 copy.54
  12.0 0.7 fusion.42
  12.9 0.7 pad_add_fusion.1
  13.7 69.8 %all-gather.4.cloned.1.call-done = bf16[1,12288,256]{2,1,0:T(8,128)(2,1)} async-done(((bf16[1,512,256]{2,1,0:T(8,128)(2,1)}), bf16[1,12288,256]{2,1,0:T(8,128)(2,1)}) %all-gather.4.cloned.1.call-update) | async-done | bytes 6291472 | tf_op jit(solution)/shard_map/all_gather | solution.py:28
  83.5 10.5 %reshape.351 = bf16[192,16384]{1,0:T(8,128)(2,1)} reshape(bf16[1,12288,256]{2,1,0:T(8,128)(2,1)} %all-gather.4.cloned.1.call-done) | data formatting | bytes 12582912 | tf_op jit(solution)/shard_map/reshape.78
  94.0 4.1 %convolution_convert_fusion.1 = bf16[16384,26]{0,1:T(8,128)(2,1)S(1)} fusion(bf16[192,16384]{1,0:T(8,128)(2,1)} %reshape.351, s32[26]{0:T(128)S(1)} %pad_add_fusion.1), kind=kOutput, calls=%fused_computation.2 | convolution fusion | flops 164008832 | bytes 7143528 | tf_op jit(solution)/shard_map/pc,hcx->hpx/dot_general | solution.py:62
  98.5 0.8 constant_dynamic-slice_fusion.2
  101.5 1.0 fusion.13
  102.6 0.9 fusion
  104.7 0.7 pad_maximum_fusion.3
  107.0 1.6 copy.78
  108.6 6.0 %all-to-all-start = ((bf16[1,24,2,64,256]{4,3,2,0,1:T(8,128)(2,1)}), bf16[1,24,2,64,256]{4,3,2,0,1:T(8,128)(2,1)S(1)}, u32[]{:S(2)}, u32[]{:S(2)}) async-start(bf16[1,24,2,64,256]{4,3,2,0,1:T(8,128)(2,1)} %bitcast.52), calls=%async_computation | async-start | bytes 3145728 | tf_op jit(solution)/shard_map/all_to_all | solution.py:128
  115.4 2.7 %fusion.12 = bf16[8,64,128]{2,1,0:T(8,128)(2,1)} fusion(bf16[8,64,8,64]{1,3,2,0:T(8,128)(2,1)} %copy-done.4, bf16[1,8,8,64,256]{4,3,2,1,0:T(8,128)(2,1)} %copy-done.5), kind=kOutput, calls=%fused_computation.33 | convolution fusion | flops 67239936 | bytes 2228224 | tf_op jit(solution)/shard_map/hiqsk,hiskd->hiqd/dot_general | solution.py:102
  118.1 66.8 %all-to-all-done = bf16[1,24,2,64,256]{4,3,2,0,1:T(8,128)(2,1)S(1)} async-done(((bf16[1,24,2,64,256]{4,3,2,0,1:T(8,128)(2,1)}), bf16[1,24,2,64,256]{4,3,2,0,1:T(8,128)(2,1)S(1)}, u32[]{:S(2)}, u32[]{:S(2)}) %all-to-all-start) | async-done | bytes 1572896 | tf_op jit(solution)/shard_map/all_to_all | solution.py:128
  184.9 0.9 copy.79
  186.2 2.6 %all-gather.6.cloned.1.call-done = bf16[24,4,64,256]{3,2,1,0:T(8,128)(2,1)} async-done(((bf16[1,4,64,256]{3,2,1,0:T(8,128)(2,1)}), bf16[24,4,64,256]{3,2,1,0:T(8,128)(2,1)}) %all-gather.6.cloned.1.call-update) | async-done | bytes 3145744 | tf_op jit(solution)/shard_map/all_gather | solution.py:142
  188.9 1.6 convert_reduce_fusion
  190.6 0.8 fusion.28
  191.3 0.8 fusion.27
  193.0 0.8 fusion.41
  (69 shorter events, 8.2 us)
Async XLA Ops:
  7.2 92.3 %copy-start = (bf16[1,512,128]{2,1,0:T(8,128)(2,1)S(1)}, bf16[1,512,128]{2,1,0:T(8,128)(2,1)}, u32[]{:S(2)}) copy-start(bf16[1,512,128]{2,1,0:T(8,128)(2,1)} %param.11) | copy-start | bytes 393220
  7.2 76.3 %all-gather.4.cloned.1.call-start = ((), (), s32[]{:S(2)}) async-start(), calls=%async_computation.1 | async-start | bytes 6553600 | tf_op jit(solution)/shard_map/all_gather | solution.py:28
  9.1 0.7 copy-start.1
  9.9 179.0 %all-gather.6.cloned.1.call-start = ((), (), s32[]{:S(2)}) async-start(), calls=%async_computation.2 | async-start | bytes 3276800 | tf_op jit(solution)/shard_map/all_gather | solution.py:142
  98.3 1.0 copy-start.2
  99.5 3.1 %copy-start.5 = (bf16[1,8,8,64,256]{4,3,2,1,0:T(8,128)(2,1)}, bf16[1,8,8,64,256]{4,3,2,1,0:T(8,128)(2,1)S(1)}, u32[]{:S(2)}) copy-start(bf16[1,8,8,64,256]{4,3,2,1,0:T(8,128)(2,1)S(1)} %broadcast_dynamic-update-slice_fusion) | copy-start | bytes 6291460
  100.6 0.9 copy-start.3
  103.5 2.2 %copy-start.4 = (bf16[8,64,8,64]{1,3,2,0:T(8,128)(2,1)}, bf16[8,64,8,64]{1,3,2,0:T(8,128)(2,1)S(1)}, u32[]{:S(2)}) copy-start(bf16[8,64,8,64]{1,3,2,0:T(8,128)(2,1)S(1)} %fusion) | copy-start | bytes 1572868
  108.6 6.7 %copy-start.6 = (s32[2]{0:T(128)S(1)}, s32[2]{0:T(128)}, u32[]{:S(2)}) copy-start(s32[2]{0:T(128)} %param.17) | copy-start | bytes 28
  108.6 76.2 %all-to-all-start = ((bf16[1,24,2,64,256]{4,3,2,0,1:T(8,128)(2,1)}), bf16[1,24,2,64,256]{4,3,2,0,1:T(8,128)(2,1)S(1)}, u32[]{:S(2)}, u32[]{:S(2)}) async-start(bf16[1,24,2,64,256]{4,3,2,0,1:T(8,128)(2,1)} %bitcast.52), calls=%async_computation | async-start | bytes 3145728 | tf_op jit(solution)/shard_map/all_to_all | solution.py:128
Sparse Core Ops, SparseCore 0:
  10.4 73.0 all-gather.3
  105.6 83.2 all-gather.5

commit v4 on v3

--- a/solution.py
+++ b/solution.py
@@ -56,13 +56,9 @@
     return_at = my_owner * slot_count + my_position
     wanted = my_owner * block_count + my_slot
     piece_blocks = piece_rows.shape[1] // BLOCK
-    grouped = piece_rows.reshape(head_count, piece_blocks, BLOCK * pair_width)
+    grouped = piece_rows.reshape(head_count, piece_blocks, BLOCK, pair_width)
     pick_ids = jnp.concatenate([wanted, glob_ids.astype(jnp.int32)])
-    pick_hot = pick_ids[:, None] == jnp.arange(piece_blocks, dtype=jnp.int32)[None, :]
-    picked = jnp.einsum(
-        "pc,hcx->hpx", pick_hot.astype(jnp.bfloat16), grouped, preferred_element_type=jnp.float32
-    ).astype(jnp.bfloat16)
-    picked = picked.reshape(head_count, block_count * rand_count + glob_count, BLOCK, pair_width)
+    picked = jnp.take(grouped, jnp.clip(pick_ids, 0, piece_blocks - 1), axis=1)
     random_pairs = picked[:, : block_count * rand_count].reshape(
         head_count, block_count, rand_count, BLOCK, pair_width
     )
@@ -136,16 +132,12 @@
     edge_out = jnp.concatenate([wide_grad[:, 0], wide_grad[:, block_count + 1]], axis=1).astype(
         jnp.bfloat16
     )
-    edge_out = edge_out.reshape(head_count, 2, BLOCK, pair_width)
+    rightward = [(i, i + 1) for i in range(seq_count - 1)]
+    leftward = [(i + 1, i) for i in range(seq_count - 1)]
+    from_left = lax.ppermute(edge_out[:, BLOCK:], "seq", rightward).astype(jnp.float32)
+    from_right = lax.ppermute(edge_out[:, :BLOCK], "seq", leftward).astype(jnp.float32)
     global_terms = jnp.sum(global_full, axis=1).astype(jnp.bfloat16)
-    shared_out = jnp.concatenate([edge_out, global_terms], axis=1)
-    shared_in = lax.all_gather(shared_out, "seq", axis=0)
-    left_in = lax.dynamic_index_in_dim(shared_in, jnp.maximum(seq_place - 1, 0), 0, keepdims=False)
-    right_in = lax.dynamic_index_in_dim(
-        shared_in, jnp.minimum(seq_place + 1, seq_count - 1), 0, keepdims=False
-    )
-    from_left = jnp.where(seq_place > 0, left_in[:, 1].astype(jnp.float32), 0.0)
-    from_right = jnp.where(seq_place < seq_count - 1, right_in[:, 0].astype(jnp.float32), 0.0)
+    global_parts = lax.all_gather(global_terms, "seq", axis=0)
     accum = wide_grad[:, 1 : block_count + 1]
     accum = accum.at[:, 0].add(from_left)
     accum = accum.at[:, block_count - 1].add(from_right)
@@ -157,7 +149,7 @@
         "cb,ecx->ebx", block_hot.astype(jnp.bfloat16), returned, preferred_element_type=jnp.float32
     )
     accum = accum + gathered.reshape(head_count, block_count, BLOCK, pair_width)
-    global_sums = jnp.sum(shared_in[:, :, 2:].astype(jnp.float32), axis=0)
+    global_sums = jnp.sum(global_parts.astype(jnp.float32), axis=0)
     at_first = (seq_place == 0).astype(jnp.float32)
     accum = accum.at[:, glob_ids].add(global_sums * at_first)
     grad_q = grad_query.reshape(head_count, row_count, head_width).astype(jnp.bfloat16)

time: 201 us -> 184 us (0.915)
  waiting for transfers between devices: 139 us -> 129 us
  local copies, waits for them, and re-layouts: 20.9 us -> 13.5 us
  starting transfers between devices: 6.05 us -> 11.5 us
  matrix products: 11.5 us -> 7.83 us
    all_to_all x1, waiting for transfers between devices: 66.8 us -> 0.01 us  [local(): lax.all_to_all(outgoing_grads, 'seq', split_axis=1, concat_axis=1, tiled=...]
    ppermute x0 -> x2, waiting for transfers between devices: none -> 47 us  [the longest x1 41.9 us: local(): lax.ppermute(edge_out[:, BLOCK:], 'seq', rightward).astype(jnp.float32)]
    another operation x1 -> x0, local copies, waits for them, and re-layouts: 10.5 us -> none
    all_gather x1, waiting for transfers between devices: 2.64 us -> 12.7 us  [local(): global_parts = lax.all_gather(global_terms, 'seq', axis=0)]
    ppermute x0 -> x2, starting transfers between devices: none -> 5.59 us  [the longest x1 3.68 us: local(): lax.ppermute(edge_out[:, BLOCK:], 'seq', rightward).astype(jnp.float32)]
    dot_general x1 -> x0, matrix products: 4.07 us -> none  [local(): jnp.einsum('pc,hcx->hpx', pick_hot.astype(jnp.bfloat16), grouped, preferr...]
    gather x0 -> x1, local copies, waits for them, and re-layouts: none -> 3.38 us  [local(): picked = jnp.take(grouped, jnp.clip(pick_ids, 0, piece_blocks - 1), axis=1)]
    unnamed x26 -> x29, local copies, waits for them, and re-layouts: 7 us -> 6.7 us
  transfers between devices with their start and end apart: 3 -> 5, of which waited for: 3 -> 4; matrix products, arithmetic and copies ran while one was open for 6% -> 6% of each run, Pallas kernels for 0% -> 0%
where the time goes in v4:
time: 184 us
  waiting for transfers between devices  129 us (70%)
  between operations  14.5 us (8%)
  local copies, waits for them, and re-layouts  13.5 us (7%)
  starting transfers between devices  11.5 us (6%)
  matrix products  7.83 us (4%)
  other arithmetic  7.67 us (4%)
    all_gather x1, waiting for transfers between devices, local(): piece_rows = lax.all_gather(paired, 'seq', axis=1, tiled=True)  69.1 us
    ppermute x1, waiting for transfers between devices, local(): lax.ppermute(edge_out[:, BLOCK:], 'seq', rightward).astype(jnp.float32)  41.9 us
    all_gather x1, waiting for transfers between devices, local(): global_parts = lax.all_gather(global_terms, 'seq', axis=0)  12.7 us
    unnamed x29, local copies, waits for them, and re-layouts  6.7 us
    all_to_all x1, starting transfers between devices, local(): lax.all_to_all(outgoing_grads, 'seq', split_axis=1, concat_axis=1, tiled=...  5.83 us
    ppermute x1, waiting for transfers between devices, local(): lax.ppermute(edge_out[:, :BLOCK], 'seq', leftward).astype(jnp.float32)  5.05 us
  transfers between devices with their start and end apart: 5, of which 4 were waited for; matrix products, arithmetic and copies ran while one was open for 6% of the time, Pallas kernels for 0%

profile of v4, /device:TPU:1, one launch (start us, length us, event | category | flops | bytes accessed | tf_op | source)
XLA Modules:
  0.0 183.9 jit_solution(743392783378445139)
XLA Ops:
  7.2 1.0 constant_dynamic-update-slice_fusion.1
  8.2 0.9 constant_dynamic-update-slice_fusion
  9.9 0.8 copy.52
  10.9 0.8 copy.54
  12.9 0.7 compare_and_fusion
  13.6 0.7 fusion.38
  14.4 69.1 %all-gather.4.cloned.1.call-done = bf16[1,12288,256]{2,1,0:T(8,128)(2,1)} async-done(((bf16[1,512,256]{2,1,0:T(8,128)(2,1)}), bf16[1,12288,256]{2,1,0:T(8,128)(2,1)}) %all-gather.4.cloned.1.call-update) | async-done | bytes 6291472 | tf_op jit(solution)/shard_map/all_gather | solution.py:28
  83.5 3.4 %gather_fusion = bf16[26,64,256]{2,1,0:T(8,128)(2,1)S(1)} fusion(bf16[192,64,256]{2,1,0:T(8,128)(2,1)} %bitcast.203, s32[1024]{0:T(1024)S(1)} %pad_clamp_fusion), kind=kCustom, calls=%fused_computation | custom fusion | bytes 1704040 | tf_op jit(solution)/shard_map/jit(_take)/gather | solution.py:61
  87.1 0.8 constant_dynamic-slice_fusion.2
  90.2 1.0 fusion.13
  91.2 0.9 fusion
  93.7 1.5 copy.77
  95.3 5.8 %all-to-all-start = ((bf16[1,24,2,64,256]{4,3,2,0,1:T(8,128)(2,1)}), bf16[1,24,2,64,256]{4,3,2,0,1:T(8,128)(2,1)S(1)}, u32[]{:S(2)}, u32[]{:S(2)}) async-start(bf16[1,24,2,64,256]{4,3,2,0,1:T(8,128)(2,1)} %bitcast.50), calls=%async_computation | async-start | bytes 3145728 | tf_op jit(solution)/shard_map/all_to_all | solution.py:124
  101.4 1.2 fusion.6
  104.2 1.2 fusion.4
  105.8 3.7 %collective-permute-start = (bf16[1,64,256]{2,1,0:T(8,128)(2,1)S(1)}, bf16[1,64,256]{2,1,0:T(8,128)(2,1)S(1)}, u32[]{:S(2)}, u32[]{:S(2)}) collective-permute-start(bf16[1,64,256]{2,1,0:T(8,128)(2,1)S(1)} %get-tuple-element.37), channel_id=1, source_target_pairs={{0,32},{32,64},{64,96},{96,128},{128,160},{160,192},{192,224},{224... | collective-permute-start | bytes 98312 | tf_op jit(solution)/shard_map/ppermute | solution.py:137
  109.5 1.1 fusion.12
  110.6 1.9 %collective-permute-start.1 = (bf16[1,64,256]{2,1,0:T(8,128)(2,1)S(1)}, bf16[1,64,256]{2,1,0:T(8,128)(2,1)S(1)}, u32[]{:S(2)}, u32[]{:S(2)}) collective-permute-start(bf16[1,64,256]{2,1,0:T(8,128)(2,1)S(1)} %get-tuple-element.36), channel_id=1, source_target_pairs={{32,0},{64,32},{96,64},{128,96},{160,128},{192,160},{224,192},{256... | collective-permute-start | bytes 98312 | tf_op jit(solution)/shard_map/ppermute | solution.py:138
  112.6 41.9 %collective-permute-done = bf16[1,64,256]{2,1,0:T(8,128)(2,1)S(1)} collective-permute-done((bf16[1,64,256]{2,1,0:T(8,128)(2,1)S(1)}, bf16[1,64,256]{2,1,0:T(8,128)(2,1)S(1)}, u32[]{:S(2)}, u32[]{:S(2)}) %collective-permute-start) | collective-permute-done | bytes 32800 | tf_op jit(solution)/shard_map/ppermute | solution.py:137
  154.5 5.1 %collective-permute-done.1 = bf16[1,64,256]{2,1,0:T(8,128)(2,1)S(1)} collective-permute-done((bf16[1,64,256]{2,1,0:T(8,128)(2,1)S(1)}, bf16[1,64,256]{2,1,0:T(8,128)(2,1)S(1)}, u32[]{:S(2)}, u32[]{:S(2)}) %collective-permute-start.1) | collective-permute-done | bytes 32800 | tf_op jit(solution)/shard_map/ppermute | solution.py:138
  159.6 12.7 %all-gather.6.cloned.1.call-done = bf16[48,64,256]{2,1,0:T(8,128)(2,1)} async-done(((bf16[2,64,256]{2,1,0:T(8,128)(2,1)}), bf16[48,64,256]{2,1,0:T(8,128)(2,1)}) %all-gather.6.cloned.1.call-update) | async-done | bytes 1572880 | tf_op jit(solution)/shard_map/all_gather | solution.py:140
  172.3 1.7 convert_reduce_fusion
  174.0 0.9 copy.78
  176.3 0.8 fusion.41
  (75 shorter events, 9.7 us)
Async XLA Ops:
  7.2 81.0 %copy-start = (bf16[1,512,128]{2,1,0:T(8,128)(2,1)S(1)}, bf16[1,512,128]{2,1,0:T(8,128)(2,1)}, u32[]{:S(2)}) copy-start(bf16[1,512,128]{2,1,0:T(8,128)(2,1)} %param.11) | copy-start | bytes 393220
  7.2 76.3 %all-gather.4.cloned.1.call-start = ((), (), s32[]{:S(2)}) async-start(), calls=%async_computation.1 | async-start | bytes 6553600 | tf_op jit(solution)/shard_map/all_gather | solution.py:28
  9.1 0.7 copy-start.1
  86.9 1.0 copy-start.2
  88.1 3.1 %copy-start.6 = (bf16[1,8,8,64,256]{4,3,2,1,0:T(8,128)(2,1)}, bf16[1,8,8,64,256]{4,3,2,1,0:T(8,128)(2,1)S(1)}, u32[]{:S(2)}) copy-start(bf16[1,8,8,64,256]{4,3,2,1,0:T(8,128)(2,1)S(1)} %broadcast_dynamic-update-slice_fusion) | copy-start | bytes 6291460
  89.3 0.9 copy-start.3
  92.1 1.0 copy-start.4
  95.3 78.7 %all-to-all-start = ((bf16[1,24,2,64,256]{4,3,2,0,1:T(8,128)(2,1)}), bf16[1,24,2,64,256]{4,3,2,0,1:T(8,128)(2,1)S(1)}, u32[]{:S(2)}, u32[]{:S(2)}) async-start(bf16[1,24,2,64,256]{4,3,2,0,1:T(8,128)(2,1)} %bitcast.50), calls=%async_computation | async-start | bytes 3145728 | tf_op jit(solution)/shard_map/all_to_all | solution.py:124
  101.1 2.9 %copy-start.8 = (s32[2]{0:T(128)S(1)}, s32[2]{0:T(128)}, u32[]{:S(2)}) copy-start(s32[2]{0:T(128)} %param.17) | copy-start | bytes 28
  101.1 71.2 %all-gather.6.cloned.1.call-start = ((), (), s32[]{:S(2)}) async-start(), calls=%async_computation.2 | async-start | bytes 1638400 | tf_op jit(solution)/shard_map/all_gather | solution.py:140
  105.5 4.0 %copy-start.7 = (bf16[1,8,8,64,256]{4,3,2,1,0:T(8,128)(2,1)S(1)}, bf16[1,8,8,64,256]{4,3,2,1,0:T(8,128)(2,1)}, u32[]{:S(2)}) copy-start(bf16[1,8,8,64,256]{4,3,2,1,0:T(8,128)(2,1)} %copy-done.6) | copy-start | bytes 6291460
  105.6 3.9 %copy-start.5 = (bf16[8,64,8,64]{1,3,2,0:T(8,128)(2,1)S(1)}, bf16[8,64,8,64]{1,3,2,0:T(8,128)(2,1)}, u32[]{:S(2)}) copy-start(bf16[8,64,8,64]{1,3,2,0:T(8,128)(2,1)} %copy-done.4) | copy-start | bytes 1572868
  105.8 48.7 %collective-permute-start = (bf16[1,64,256]{2,1,0:T(8,128)(2,1)S(1)}, bf16[1,64,256]{2,1,0:T(8,128)(2,1)S(1)}, u32[]{:S(2)}, u32[]{:S(2)}) collective-permute-start(bf16[1,64,256]{2,1,0:T(8,128)(2,1)S(1)} %get-tuple-element.37), channel_id=1, source_target_pairs={{0,32},{32,64},{64,96},{96,128},{128,160},{160,192},{192,224},{224... | collective-permute-start | bytes 98312 | tf_op jit(solution)/shard_map/ppermute | solution.py:137
  110.6 49.0 %collective-permute-start.1 = (bf16[1,64,256]{2,1,0:T(8,128)(2,1)S(1)}, bf16[1,64,256]{2,1,0:T(8,128)(2,1)S(1)}, u32[]{:S(2)}, u32[]{:S(2)}) collective-permute-start(bf16[1,64,256]{2,1,0:T(8,128)(2,1)S(1)} %get-tuple-element.36), channel_id=1, source_target_pairs={{32,0},{64,32},{96,64},{128,96},{160,128},{192,160},{224,192},{256... | collective-permute-start | bytes 98312 | tf_op jit(solution)/shard_map/ppermute | solution.py:138
Sparse Core Ops, SparseCore 0:
  10.4 73.0 all-gather.3
  104.9 67.3 all-gather.5

commit v5 on v4

--- a/solution.py
+++ b/solution.py
@@ -3,12 +3,13 @@
 import jax
 import jax.numpy as jnp
 from jax import lax
-from jax.sharding import PartitionSpec as P
+from jax.sharding import Mesh, PartitionSpec as P
 
 BLOCK = 64
 
 
 NEG_FILL = -1e30
+SEQ = ("sz", "sc")
 
 
 def local(queries, keys, values, grad_out, rand_owner, rand_slot, glob_ids):
@@ -16,8 +17,10 @@
     block_count = row_count // BLOCK
     rand_count = rand_owner.shape[1]
     glob_count = glob_ids.shape[0]
-    seq_count = lax.axis_size("seq")
-    seq_place = lax.axis_index("seq")
+    core_count = lax.axis_size("sc")
+    core_place = lax.axis_index("sc")
+    seq_count = lax.axis_size("sz") * core_count
+    seq_place = lax.axis_index("sz") * core_count + core_place
     slot_count = min(
         block_count, max(2, (2 * block_count * rand_count + seq_count - 1) // seq_count)
     )
@@ -25,20 +28,42 @@
     score_scale = 1.0 / math.sqrt(head_width)
     paired = jnp.concatenate([keys, values], axis=2)
     paired_blocks = paired.reshape(head_count, block_count, BLOCK, pair_width)
-    piece_rows = lax.all_gather(paired, "seq", axis=1, tiled=True)
-    row_start = seq_place * row_count
-    edge_before = lax.dynamic_slice_in_dim(piece_rows, row_start - BLOCK, BLOCK, axis=1)
-    edge_after = lax.dynamic_slice_in_dim(piece_rows, row_start + row_count, BLOCK, axis=1)
-    widened = jnp.concatenate([edge_before, paired, edge_after], axis=1)
-    widened = widened.reshape(head_count, block_count + 2, BLOCK, pair_width)
+    owners_all = rand_owner.reshape(seq_count, block_count * rand_count)
+    slots_all = rand_slot.reshape(seq_count, block_count * rand_count)
+    total_blocks = seq_count * block_count
+
+    def pick_list(place):
+        owner_now = lax.dynamic_index_in_dim(owners_all, place, 0, keepdims=False)
+        slot_now = lax.dynamic_index_in_dim(slots_all, place, 0, keepdims=False)
+        edge_ids = place * block_count + jnp.array([-1, block_count], jnp.int32)
+        ids = jnp.concatenate([owner_now * block_count + slot_now, glob_ids.astype(jnp.int32), edge_ids])
+        return jnp.clip(ids, 0, total_blocks - 1)
+
+    def core_of(ids):
+        return (ids // block_count) % core_count
+
+    def row_of(ids):
+        return (ids // block_count // core_count) * block_count + ids % block_count
+
+    mine_ids = pick_list(seq_place)
+    sibling_ids = pick_list(seq_place - core_place + (1 - core_place))
+    core_rows = lax.all_gather(paired_blocks, "sz", axis=1, tiled=True)
+    for_me = jnp.take(core_rows, row_of(mine_ids), axis=1)
+    for_sibling = jnp.take(core_rows, row_of(sibling_ids), axis=1)
+    from_sibling = lax.ppermute(for_sibling, "sc", [(0, 1), (1, 0)])
+    picked = jnp.where(
+        (core_of(mine_ids) == core_place)[None, :, None, None], for_me, from_sibling
+    )
+    pick_count = block_count * rand_count + glob_count
+    widened = jnp.concatenate(
+        [picked[:, pick_count : pick_count + 1], paired_blocks, picked[:, pick_count + 1 :]], axis=1
+    )
     window_pairs = jnp.stack(
         [widened[:, offset : offset + block_count] for offset in range(3)], axis=2
     )
     global_block = seq_place * block_count + jnp.arange(block_count, dtype=jnp.int32)
     window_ids = global_block[:, None] + jnp.arange(-1, 2, dtype=jnp.int32)[None, :]
     window_ok = (window_ids >= 0) & (window_ids < seq_count * block_count)
-    owners_all = rand_owner.reshape(seq_count, block_count * rand_count)
-    slots_all = rand_slot.reshape(seq_count, block_count * rand_count)
     owner_hot = (
         owners_all[:, :, None] == jnp.arange(seq_count, dtype=jnp.int32)[None, None, :]
     ).astype(jnp.int32)
@@ -55,14 +80,10 @@
     my_position = lax.dynamic_index_in_dim(position, seq_place, 0, keepdims=False)
     return_at = my_owner * slot_count + my_position
     wanted = my_owner * block_count + my_slot
-    piece_blocks = piece_rows.shape[1] // BLOCK
-    grouped = piece_rows.reshape(head_count, piece_blocks, BLOCK, pair_width)
-    pick_ids = jnp.concatenate([wanted, glob_ids.astype(jnp.int32)])
-    picked = jnp.take(grouped, jnp.clip(pick_ids, 0, piece_blocks - 1), axis=1)
     random_pairs = picked[:, : block_count * rand_count].reshape(
         head_count, block_count, rand_count, BLOCK, pair_width
     )
-    global_pairs = picked[:, block_count * rand_count :]
+    global_pairs = picked[:, block_count * rand_count : pick_count]
     global_wide = jnp.broadcast_to(
         global_pairs[:, None], (head_count, block_count, glob_count, BLOCK, pair_width)
     )
@@ -121,7 +142,7 @@
         "ti,hix->htx", send_hot.astype(jnp.bfloat16), random_terms, preferred_element_type=jnp.float32
     ).astype(jnp.bfloat16)
     outgoing_grads = outgoing_grads.reshape(head_count, seq_count, slot_count, BLOCK, pair_width)
-    returned = lax.all_to_all(outgoing_grads, "seq", split_axis=1, concat_axis=1, tiled=True)
+    returned = lax.all_to_all(outgoing_grads, SEQ, split_axis=1, concat_axis=1, tiled=True)
     window_terms = key_terms(0, 3)
     global_full = key_terms(3 + rand_count, 3 + rand_count + glob_count)
     wide_grad = jnp.pad(window_terms[:, :, 0], ((0, 0), (0, 2), (0, 0), (0, 0)))
@@ -134,10 +155,10 @@
     )
     rightward = [(i, i + 1) for i in range(seq_count - 1)]
     leftward = [(i + 1, i) for i in range(seq_count - 1)]
-    from_left = lax.ppermute(edge_out[:, BLOCK:], "seq", rightward).astype(jnp.float32)
-    from_right = lax.ppermute(edge_out[:, :BLOCK], "seq", leftward).astype(jnp.float32)
+    from_left = lax.ppermute(edge_out[:, BLOCK:], SEQ, rightward).astype(jnp.float32)
+    from_right = lax.ppermute(edge_out[:, :BLOCK], SEQ, leftward).astype(jnp.float32)
     global_terms = jnp.sum(global_full, axis=1).astype(jnp.bfloat16)
-    global_parts = lax.all_gather(global_terms, "seq", axis=0)
+    global_parts = lax.all_gather(global_terms, SEQ, axis=0)
     accum = wide_grad[:, 1 : block_count + 1]
     accum = accum.at[:, 0].add(from_left)
     accum = accum.at[:, block_count - 1].add(from_right)
@@ -159,18 +180,15 @@
 
 
 def solution(mesh):
+    seq_size = mesh.shape["seq"]
+    core_size = 2
+    devices = mesh.devices.reshape(seq_size // core_size, core_size, mesh.shape["head"])
+    split_mesh = Mesh(devices, ("sz", "sc", "head"))
+    rows = P("head", SEQ, None)
     return jax.shard_map(
         local,
-        mesh=mesh,
-        in_specs=(
-            P("head", "seq", None),
-            P("head", "seq", None),
-            P("head", "seq", None),
-            P("head", "seq", None),
-            P(),
-            P(),
-            P(),
-        ),
-        out_specs=(P("head", "seq", None), P("head", "seq", None), P("head", "seq", None)),
+        mesh=split_mesh,
+        in_specs=(rows, rows, rows, rows, P(), P(), P()),
+        out_specs=(rows, rows, rows),
         check_vma=False,
     )

time: 184 us -> 187 us (1.016)
  starting transfers between devices: 11.5 us -> 21.5 us
  waiting for transfers between devices: 129 us -> 120 us
    ppermute x2 -> x3, starting transfers between devices: 5.59 us -> 15.7 us  [the longest x1 10.1 us: local(): from_sibling = lax.ppermute(for_sibling, 'sc', [(0, 1), (1, 0)])]
    all_gather x2, waiting for transfers between devices: 81.8 us -> 73.1 us  [the longest x1 60.3 us: local(): core_rows = lax.all_gather(paired_blocks, 'sz', axis=1, tiled=True)]
    gather x1 -> x2, local copies, waits for them, and re-layouts: 3.38 us -> 4.99 us  [the longest x1 2.49 us: local(): for_me = jnp.take(core_rows, row_of(mine_ids), axis=1)]
    unnamed x29 -> x28, local copies, waits for them, and re-layouts: 6.7 us -> 7.37 us
    ppermute x2 -> x3, waiting for transfers between devices: 47 us -> 46.8 us  [the longest x1 41.8 us: local(): lax.ppermute(edge_out[:, BLOCK:], SEQ, rightward).astype(jnp.float32)]
  transfers between devices with their start and end apart: 5 -> 6, of which waited for: 4 -> 4; matrix products, arithmetic and copies ran while one was open for 6% -> 8% of each run, Pallas kernels for 0% -> 0%
where the time goes in v5:
time: 187 us
  waiting for transfers between devices  120 us (64%)
  starting transfers between devices  21.5 us (11%)
  local copies, waits for them, and re-layouts  15 us (8%)
  between operations  14.6 us (8%)
  other arithmetic  7.92 us (4%)
  matrix products  7.82 us (4%)
    all_gather x1, waiting for transfers between devices, local(): core_rows = lax.all_gather(paired_blocks, 'sz', axis=1, tiled=True)  60.3 us
    ppermute x1, waiting for transfers between devices, local(): lax.ppermute(edge_out[:, BLOCK:], SEQ, rightward).astype(jnp.float32)  41.8 us
    all_gather x1, waiting for transfers between devices, local(): global_parts = lax.all_gather(global_terms, SEQ, axis=0)  12.8 us
    ppermute x1, starting transfers between devices, local(): from_sibling = lax.ppermute(for_sibling, 'sc', [(0, 1), (1, 0)])  10.1 us
    unnamed x28, local copies, waits for them, and re-layouts  7.37 us
    all_to_all x1, starting transfers between devices, local(): lax.all_to_all(outgoing_grads, SEQ, split_axis=1, concat_axis=1, tiled=True)  5.71 us
    ppermute x1, waiting for transfers between devices, local(): lax.ppermute(edge_out[:, :BLOCK], SEQ, leftward).astype(jnp.float32)  5.06 us
  transfers between devices with their start and end apart: 6, of which 4 were waited for; matrix products, arithmetic and copies ran while one was open for 8% of the time, Pallas kernels for 0%

profile of v5, /device:TPU:1, one launch (start us, length us, event | category | flops | bytes accessed | tf_op | source)
XLA Modules:
  0.0 186.7 jit_solution(8218763468108003686)
XLA Ops:
  7.2 1.0 constant_dynamic-update-slice_fusion.1
  8.2 0.9 constant_dynamic-update-slice_fusion
  9.9 0.8 copy.56
  10.9 0.8 copy.58
  13.6 0.8 fusion.42
  14.4 60.3 %all-gather.4.cloned.1.call-done = bf16[1,96,64,256]{3,2,0,1:T(8,128)(2,1)} async-done(((bf16[1,8,64,256]{3,2,0,1:T(8,128)(2,1)}), bf16[1,96,64,256]{3,2,0,1:T(8,128)(2,1)}) %all-gather.4.cloned.1.call-update) | async-done | bytes 3145744 | tf_op jit(solution)/shard_map/all_gather | solution.py:50
  74.6 2.5 %gather_fusion.1 = bf16[28,64,256]{2,1,0:T(8,128)(2,1)S(1)} fusion(bf16[96,64,256]{2,1,0:T(8,128)(2,1)} %bitcast.199, s32[1024]{0:T(1024)S(1)} %pad_clamp_fusion), kind=kCustom, calls=%fused_computation.1.clone | custom fusion | bytes 1835120 | tf_op jit(solution)/shard_map/jit(_take)/gather | solution.py:52
  77.3 10.1 %collective-permute-start = (bf16[1,28,64,256]{3,2,1,0:T(8,128)(2,1)S(1)}, bf16[1,28,64,256]{3,2,1,0:T(8,128)(2,1)S(1)}, u32[]{:S(2)}, u32[]{:S(2)}) collective-permute-start(bf16[1,28,64,256]{3,2,1,0:T(8,128)(2,1)S(1)} %bitcast_select_fusion), channel_id=1, source_target_pairs={{0,32},{32,0},{1,33},{33,1},{2,34},{34,2},{3,35},{35,3},{4,36},{36... | collective-permute-start | bytes 2752520 | tf_op jit(solution)/shard_map/ppermute | solution.py:53
  87.5 2.5 %gather_fusion = bf16[28,64,256]{2,1,0:T(8,128)(2,1)S(1)} fusion(bf16[96,64,256]{2,1,0:T(8,128)(2,1)} %bitcast.200, s32[1024]{0:T(1024)S(1)} %pad_clamp_fusion.1), kind=kCustom, calls=%fused_computation.clone | custom fusion | bytes 1835120 | tf_op jit(solution)/shard_map/jit(_take)/gather | solution.py:51
  93.2 1.0 fusion.13
  94.3 0.9 fusion
  96.8 1.5 copy.84
  98.3 5.7 %all-to-all-start = ((bf16[1,24,2,64,256]{4,3,2,0,1:T(8,128)(2,1)}), bf16[1,24,2,64,256]{4,3,2,0,1:T(8,128)(2,1)S(1)}, u32[]{:S(2)}, u32[]{:S(2)}) async-start(bf16[1,24,2,64,256]{4,3,2,0,1:T(8,128)(2,1)} %bitcast.50), calls=%async_computation | async-start | bytes 3145728 | tf_op jit(solution)/shard_map/all_to_all | solution.py:145
  104.3 1.2 fusion.6
  107.2 1.2 fusion.4
  108.7 3.7 %collective-permute-start.1 = (bf16[1,64,256]{2,1,0:T(8,128)(2,1)S(1)}, bf16[1,64,256]{2,1,0:T(8,128)(2,1)S(1)}, u32[]{:S(2)}, u32[]{:S(2)}) collective-permute-start(bf16[1,64,256]{2,1,0:T(8,128)(2,1)S(1)} %get-tuple-element.46), channel_id=1, source_target_pairs={{0,32},{32,64},{64,96},{96,128},{128,160},{160,192},{192,224},{224... | collective-permute-start | bytes 98312 | tf_op jit(solution)/shard_map/ppermute | solution.py:158
  112.4 1.1 fusion.12
  113.5 1.9 %collective-permute-start.2 = (bf16[1,64,256]{2,1,0:T(8,128)(2,1)S(1)}, bf16[1,64,256]{2,1,0:T(8,128)(2,1)S(1)}, u32[]{:S(2)}, u32[]{:S(2)}) collective-permute-start(bf16[1,64,256]{2,1,0:T(8,128)(2,1)S(1)} %get-tuple-element.45), channel_id=1, source_target_pairs={{32,0},{64,32},{96,64},{128,96},{160,128},{192,160},{224,192},{256... | collective-permute-start | bytes 98312 | tf_op jit(solution)/shard_map/ppermute | solution.py:159
  115.5 41.8 %collective-permute-done.1 = bf16[1,64,256]{2,1,0:T(8,128)(2,1)S(1)} collective-permute-done((bf16[1,64,256]{2,1,0:T(8,128)(2,1)S(1)}, bf16[1,64,256]{2,1,0:T(8,128)(2,1)S(1)}, u32[]{:S(2)}, u32[]{:S(2)}) %collective-permute-start.1) | collective-permute-done | bytes 32800 | tf_op jit(solution)/shard_map/ppermute | solution.py:158
  157.3 5.1 %collective-permute-done.2 = bf16[1,64,256]{2,1,0:T(8,128)(2,1)S(1)} collective-permute-done((bf16[1,64,256]{2,1,0:T(8,128)(2,1)S(1)}, bf16[1,64,256]{2,1,0:T(8,128)(2,1)S(1)}, u32[]{:S(2)}, u32[]{:S(2)}) %collective-permute-start.2) | collective-permute-done | bytes 32800 | tf_op jit(solution)/shard_map/ppermute | solution.py:159
  162.4 12.8 %all-gather.6.cloned.1.call-done = bf16[48,64,256]{2,1,0:T(8,128)(2,1)} async-done(((bf16[2,64,256]{2,1,0:T(8,128)(2,1)}), bf16[48,64,256]{2,1,0:T(8,128)(2,1)}) %all-gather.6.cloned.1.call-update) | async-done | bytes 1572880 | tf_op jit(solution)/shard_map/all_gather | solution.py:161
  175.2 1.7 convert_reduce_fusion
  176.8 0.9 copy.85
  179.1 0.8 fusion.46
  (81 shorter events, 11.3 us)
Async XLA Ops:
  7.2 84.0 %copy-start = (bf16[1,512,128]{2,1,0:T(8,128)(2,1)S(1)}, bf16[1,512,128]{2,1,0:T(8,128)(2,1)}, u32[]{:S(2)}) copy-start(bf16[1,512,128]{2,1,0:T(8,128)(2,1)} %param.15) | copy-start | bytes 393220
  7.2 67.4 %all-gather.4.cloned.1.call-start = ((), (), s32[]{:S(2)}) async-start(), calls=%async_computation.1 | async-start | bytes 3407872 | tf_op jit(solution)/shard_map/all_gather | solution.py:50
  9.1 0.7 copy-start.1
  77.3 12.8 %collective-permute-start = (bf16[1,28,64,256]{3,2,1,0:T(8,128)(2,1)S(1)}, bf16[1,28,64,256]{3,2,1,0:T(8,128)(2,1)S(1)}, u32[]{:S(2)}, u32[]{:S(2)}) collective-permute-start(bf16[1,28,64,256]{3,2,1,0:T(8,128)(2,1)S(1)} %bitcast_select_fusion), channel_id=1, source_target_pairs={{0,32},{32,0},{1,33},{33,1},{2,34},{34,2},{3,35},{35,3},{4,36},{36... | collective-permute-start | bytes 2752520 | tf_op jit(solution)/shard_map/ppermute | solution.py:53
  90.0 1.0 copy-start.2
  91.2 3.1 %copy-start.6 = (bf16[1,8,8,64,256]{4,3,2,1,0:T(8,128)(2,1)}, bf16[1,8,8,64,256]{4,3,2,1,0:T(8,128)(2,1)S(1)}, u32[]{:S(2)}) copy-start(bf16[1,8,8,64,256]{4,3,2,1,0:T(8,128)(2,1)S(1)} %broadcast_dynamic-update-slice_fusion) | copy-start | bytes 6291460
  92.3 0.9 copy-start.3
  95.2 1.0 copy-start.4
  98.3 78.5 %all-to-all-start = ((bf16[1,24,2,64,256]{4,3,2,0,1:T(8,128)(2,1)}), bf16[1,24,2,64,256]{4,3,2,0,1:T(8,128)(2,1)S(1)}, u32[]{:S(2)}, u32[]{:S(2)}) async-start(bf16[1,24,2,64,256]{4,3,2,0,1:T(8,128)(2,1)} %bitcast.50), calls=%async_computation | async-start | bytes 3145728 | tf_op jit(solution)/shard_map/all_to_all | solution.py:145
  104.0 2.9 %copy-start.8 = (s32[2]{0:T(128)S(1)}, s32[2]{0:T(128)}, u32[]{:S(2)}) copy-start(s32[2]{0:T(128)} %param.21) | copy-start | bytes 28
  104.0 71.1 %all-gather.6.cloned.1.call-start = ((), (), s32[]{:S(2)}) async-start(), calls=%async_computation.2 | async-start | bytes 1638400 | tf_op jit(solution)/shard_map/all_gather | solution.py:161
  108.4 4.0 %copy-start.7 = (bf16[1,8,8,64,256]{4,3,2,1,0:T(8,128)(2,1)S(1)}, bf16[1,8,8,64,256]{4,3,2,1,0:T(8,128)(2,1)}, u32[]{:S(2)}) copy-start(bf16[1,8,8,64,256]{4,3,2,1,0:T(8,128)(2,1)} %copy-done.6) | copy-start | bytes 6291460
  108.5 3.9 %copy-start.5 = (bf16[8,64,8,64]{1,3,2,0:T(8,128)(2,1)S(1)}, bf16[8,64,8,64]{1,3,2,0:T(8,128)(2,1)}, u32[]{:S(2)}) copy-start(bf16[8,64,8,64]{1,3,2,0:T(8,128)(2,1)} %copy-done.4) | copy-start | bytes 1572868
  108.7 48.6 %collective-permute-start.1 = (bf16[1,64,256]{2,1,0:T(8,128)(2,1)S(1)}, bf16[1,64,256]{2,1,0:T(8,128)(2,1)S(1)}, u32[]{:S(2)}, u32[]{:S(2)}) collective-permute-start(bf16[1,64,256]{2,1,0:T(8,128)(2,1)S(1)} %get-tuple-element.46), channel_id=1, source_target_pairs={{0,32},{32,64},{64,96},{96,128},{128,160},{160,192},{192,224},{224... | collective-permute-start | bytes 98312 | tf_op jit(solution)/shard_map/ppermute | solution.py:158
  113.5 48.8 %collective-permute-start.2 = (bf16[1,64,256]{2,1,0:T(8,128)(2,1)S(1)}, bf16[1,64,256]{2,1,0:T(8,128)(2,1)S(1)}, u32[]{:S(2)}, u32[]{:S(2)}) collective-permute-start(bf16[1,64,256]{2,1,0:T(8,128)(2,1)S(1)} %get-tuple-element.45), channel_id=1, source_target_pairs={{32,0},{64,32},{96,64},{128,96},{160,128},{192,160},{224,192},{256... | collective-permute-start | bytes 98312 | tf_op jit(solution)/shard_map/ppermute | solution.py:159
Sparse Core Ops, SparseCore 0:
  10.4 64.1 all-gather.3
  107.9 67.2 all-gather.5

commit v6 on v5

--- a/solution.py
+++ b/solution.py
@@ -39,21 +39,14 @@
         ids = jnp.concatenate([owner_now * block_count + slot_now, glob_ids.astype(jnp.int32), edge_ids])
         return jnp.clip(ids, 0, total_blocks - 1)
 
-    def core_of(ids):
-        return (ids // block_count) % core_count
-
     def row_of(ids):
-        return (ids // block_count // core_count) * block_count + ids % block_count
+        seq_of = ids // block_count
+        order_of = (seq_of % core_count) * (seq_count // core_count) + seq_of // core_count
+        return order_of * block_count + ids % block_count
 
     mine_ids = pick_list(seq_place)
-    sibling_ids = pick_list(seq_place - core_place + (1 - core_place))
-    core_rows = lax.all_gather(paired_blocks, "sz", axis=1, tiled=True)
-    for_me = jnp.take(core_rows, row_of(mine_ids), axis=1)
-    for_sibling = jnp.take(core_rows, row_of(sibling_ids), axis=1)
-    from_sibling = lax.ppermute(for_sibling, "sc", [(0, 1), (1, 0)])
-    picked = jnp.where(
-        (core_of(mine_ids) == core_place)[None, :, None, None], for_me, from_sibling
-    )
+    all_rows = lax.all_gather(paired_blocks, ("sc", "sz"), axis=1, tiled=True)
+    picked = jnp.take(all_rows, row_of(mine_ids), axis=1)
     pick_count = block_count * rand_count + glob_count
     widened = jnp.concatenate(
         [picked[:, pick_count : pick_count + 1], paired_blocks, picked[:, pick_count + 1 :]], axis=1

time: 187 us -> 184 us (0.984)
  starting transfers between devices: 21.5 us -> 11.5 us
  waiting for transfers between devices: 120 us -> 128 us
    ppermute x1 -> x0, starting transfers between devices: 10.1 us -> none  [local(): from_sibling = lax.ppermute(for_sibling, 'sc', [(0, 1), (1, 0)])]
    all_gather x1, waiting for transfers between devices: 60.3 us -> 68.4 us  [local(): all_rows = lax.all_gather(paired_blocks, ('sc', 'sz'), axis=1, tiled=True)]
    gather x2 -> x1, local copies, waits for them, and re-layouts: 4.99 us -> 3.39 us  [local(): picked = jnp.take(all_rows, row_of(mine_ids), axis=1)]
    unnamed x28 -> x27, local copies, waits for them, and re-layouts: 7.37 us -> 7.35 us
  transfers between devices with their start and end apart: 6 -> 5, of which waited for: 4 -> 4; matrix products, arithmetic and copies ran while one was open for 8% -> 7% of each run, Pallas kernels for 0% -> 0%
where the time goes in v6:
time: 184 us
  waiting for transfers between devices  128 us (70%)
  between operations  14.5 us (8%)
  local copies, waits for them, and re-layouts  13.4 us (7%)
  starting transfers between devices  11.5 us (6%)
  other arithmetic  8.4 us (5%)
  matrix products  7.82 us (4%)
    all_gather x1, waiting for transfers between devices, local(): all_rows = lax.all_gather(paired_blocks, ('sc', 'sz'), axis=1, tiled=True)  68.4 us
    ppermute x1, waiting for transfers between devices, local(): lax.ppermute(edge_out[:, BLOCK:], SEQ, rightward).astype(jnp.float32)  41.9 us
    all_gather x1, waiting for transfers between devices, local(): global_parts = lax.all_gather(global_terms, SEQ, axis=0)  12.9 us
    unnamed x27, local copies, waits for them, and re-layouts  7.35 us
    all_to_all x1, starting transfers between devices, local(): lax.all_to_all(outgoing_grads, SEQ, split_axis=1, concat_axis=1, tiled=True)  5.83 us
    ppermute x1, waiting for transfers between devices, local(): lax.ppermute(edge_out[:, :BLOCK], SEQ, leftward).astype(jnp.float32)  5.07 us
  transfers between devices with their start and end apart: 5, of which 4 were waited for; matrix products, arithmetic and copies ran while one was open for 7% of the time, Pallas kernels for 0%

profile of v6, /device:TPU:1, one launch (start us, length us, event | category | flops | bytes accessed | tf_op | source)
XLA Modules:
  0.0 183.9 jit_solution(3750121106351268149)
XLA Ops:
  7.2 1.0 constant_dynamic-update-slice_fusion.1
  8.2 0.9 constant_dynamic-update-slice_fusion
  9.9 0.8 copy.51
  10.9 0.8 copy.53
  12.0 0.7 fusion.51
  13.5 0.8 compare_and_fusion
  14.3 0.8 fusion.45
  15.1 68.4 %all-gather.4.cloned.1.call-done = bf16[1,192,64,256]{3,2,0,1:T(8,128)(2,1)} async-done(((bf16[1,8,64,256]{3,2,0,1:T(8,128)(2,1)}), bf16[1,192,64,256]{3,2,0,1:T(8,128)(2,1)}) %all-gather.4.cloned.1.call-update) | async-done | bytes 6291472 | tf_op jit(solution)/shard_map/all_gather | solution.py:48
  83.5 3.4 %gather_fusion = bf16[28,64,256]{2,1,0:T(8,128)(2,1)S(1)} fusion(bf16[192,64,256]{2,1,0:T(8,128)(2,1)} %bitcast.203, s32[1024]{0:T(1024)S(1)} %pad_clamp_fusion), kind=kCustom, calls=%fused_computation | custom fusion | bytes 1835120 | tf_op jit(solution)/shard_map/jit(_take)/gather | solution.py:49
  90.1 1.0 fusion.13
  91.1 0.9 fusion
  93.6 1.5 copy.76
  95.1 5.8 %all-to-all-start = ((bf16[1,24,2,64,256]{4,3,2,0,1:T(8,128)(2,1)}), bf16[1,24,2,64,256]{4,3,2,0,1:T(8,128)(2,1)S(1)}, u32[]{:S(2)}, u32[]{:S(2)}) async-start(bf16[1,24,2,64,256]{4,3,2,0,1:T(8,128)(2,1)} %bitcast.51), calls=%async_computation | async-start | bytes 3145728 | tf_op jit(solution)/shard_map/all_to_all | solution.py:138
  101.3 1.2 fusion.6
  104.1 1.2 fusion.4
  105.7 3.7 %collective-permute-start = (bf16[1,64,256]{2,1,0:T(8,128)(2,1)S(1)}, bf16[1,64,256]{2,1,0:T(8,128)(2,1)S(1)}, u32[]{:S(2)}, u32[]{:S(2)}) collective-permute-start(bf16[1,64,256]{2,1,0:T(8,128)(2,1)S(1)} %get-tuple-element.37), channel_id=1, source_target_pairs={{0,32},{32,64},{64,96},{96,128},{128,160},{160,192},{192,224},{224... | collective-permute-start | bytes 98312 | tf_op jit(solution)/shard_map/ppermute | solution.py:151
  109.4 1.1 fusion.12
  110.5 1.9 %collective-permute-start.1 = (bf16[1,64,256]{2,1,0:T(8,128)(2,1)S(1)}, bf16[1,64,256]{2,1,0:T(8,128)(2,1)S(1)}, u32[]{:S(2)}, u32[]{:S(2)}) collective-permute-start(bf16[1,64,256]{2,1,0:T(8,128)(2,1)S(1)} %get-tuple-element.36), channel_id=1, source_target_pairs={{32,0},{64,32},{96,64},{128,96},{160,128},{192,160},{224,192},{256... | collective-permute-start | bytes 98312 | tf_op jit(solution)/shard_map/ppermute | solution.py:152
  112.5 41.9 %collective-permute-done = bf16[1,64,256]{2,1,0:T(8,128)(2,1)S(1)} collective-permute-done((bf16[1,64,256]{2,1,0:T(8,128)(2,1)S(1)}, bf16[1,64,256]{2,1,0:T(8,128)(2,1)S(1)}, u32[]{:S(2)}, u32[]{:S(2)}) %collective-permute-start) | collective-permute-done | bytes 32800 | tf_op jit(solution)/shard_map/ppermute | solution.py:151
  154.4 5.1 %collective-permute-done.1 = bf16[1,64,256]{2,1,0:T(8,128)(2,1)S(1)} collective-permute-done((bf16[1,64,256]{2,1,0:T(8,128)(2,1)S(1)}, bf16[1,64,256]{2,1,0:T(8,128)(2,1)S(1)}, u32[]{:S(2)}, u32[]{:S(2)}) %collective-permute-start.1) | collective-permute-done | bytes 32800 | tf_op jit(solution)/shard_map/ppermute | solution.py:152
  159.5 12.9 %all-gather.6.cloned.1.call-done = bf16[48,64,256]{2,1,0:T(8,128)(2,1)} async-done(((bf16[2,64,256]{2,1,0:T(8,128)(2,1)}), bf16[48,64,256]{2,1,0:T(8,128)(2,1)}) %all-gather.6.cloned.1.call-update) | async-done | bytes 1572880 | tf_op jit(solution)/shard_map/all_gather | solution.py:154
  172.3 1.7 convert_reduce_fusion
  174.0 0.9 copy.77
  176.3 0.8 fusion.50
  (75 shorter events, 10.3 us)
Async XLA Ops:
  7.2 80.9 %copy-start = (bf16[1,512,128]{2,1,0:T(8,128)(2,1)S(1)}, bf16[1,512,128]{2,1,0:T(8,128)(2,1)}, u32[]{:S(2)}) copy-start(bf16[1,512,128]{2,1,0:T(8,128)(2,1)} %param.12) | copy-start | bytes 393220
  7.2 76.3 %all-gather.4.cloned.1.call-start = ((), (), s32[]{:S(2)}) async-start(), calls=%async_computation.1 | async-start | bytes 6553600 | tf_op jit(solution)/shard_map/all_gather | solution.py:48
  9.1 0.7 copy-start.1
  86.9 1.0 copy-start.2
  88.0 3.1 %copy-start.6 = (bf16[1,8,8,64,256]{4,3,2,1,0:T(8,128)(2,1)}, bf16[1,8,8,64,256]{4,3,2,1,0:T(8,128)(2,1)S(1)}, u32[]{:S(2)}) copy-start(bf16[1,8,8,64,256]{4,3,2,1,0:T(8,128)(2,1)S(1)} %broadcast_dynamic-update-slice_fusion) | copy-start | bytes 6291460
  89.2 0.9 copy-start.3
  92.0 1.0 copy-start.4
  95.1 78.9 %all-to-all-start = ((bf16[1,24,2,64,256]{4,3,2,0,1:T(8,128)(2,1)}), bf16[1,24,2,64,256]{4,3,2,0,1:T(8,128)(2,1)S(1)}, u32[]{:S(2)}, u32[]{:S(2)}) async-start(bf16[1,24,2,64,256]{4,3,2,0,1:T(8,128)(2,1)} %bitcast.51), calls=%async_computation | async-start | bytes 3145728 | tf_op jit(solution)/shard_map/all_to_all | solution.py:138
  101.0 2.9 %copy-start.8 = (s32[2]{0:T(128)S(1)}, s32[2]{0:T(128)}, u32[]{:S(2)}) copy-start(s32[2]{0:T(128)} %param.18) | copy-start | bytes 28
  101.0 71.3 %all-gather.6.cloned.1.call-start = ((), (), s32[]{:S(2)}) async-start(), calls=%async_computation.2 | async-start | bytes 1638400 | tf_op jit(solution)/shard_map/all_gather | solution.py:154
  105.4 4.0 %copy-start.7 = (bf16[1,8,8,64,256]{4,3,2,1,0:T(8,128)(2,1)S(1)}, bf16[1,8,8,64,256]{4,3,2,1,0:T(8,128)(2,1)}, u32[]{:S(2)}) copy-start(bf16[1,8,8,64,256]{4,3,2,1,0:T(8,128)(2,1)} %copy-done.6) | copy-start | bytes 6291460
  105.5 3.9 %copy-start.5 = (bf16[8,64,8,64]{1,3,2,0:T(8,128)(2,1)S(1)}, bf16[8,64,8,64]{1,3,2,0:T(8,128)(2,1)}, u32[]{:S(2)}) copy-start(bf16[8,64,8,64]{1,3,2,0:T(8,128)(2,1)} %copy-done.4) | copy-start | bytes 1572868
  105.7 48.7 %collective-permute-start = (bf16[1,64,256]{2,1,0:T(8,128)(2,1)S(1)}, bf16[1,64,256]{2,1,0:T(8,128)(2,1)S(1)}, u32[]{:S(2)}, u32[]{:S(2)}) collective-permute-start(bf16[1,64,256]{2,1,0:T(8,128)(2,1)S(1)} %get-tuple-element.37), channel_id=1, source_target_pairs={{0,32},{32,64},{64,96},{96,128},{128,160},{160,192},{192,224},{224... | collective-permute-start | bytes 98312 | tf_op jit(solution)/shard_map/ppermute | solution.py:151
  110.5 49.0 %collective-permute-start.1 = (bf16[1,64,256]{2,1,0:T(8,128)(2,1)S(1)}, bf16[1,64,256]{2,1,0:T(8,128)(2,1)S(1)}, u32[]{:S(2)}, u32[]{:S(2)}) collective-permute-start(bf16[1,64,256]{2,1,0:T(8,128)(2,1)S(1)} %get-tuple-element.36), channel_id=1, source_target_pairs={{32,0},{64,32},{96,64},{128,96},{160,128},{192,160},{224,192},{256... | collective-permute-start | bytes 98312 | tf_op jit(solution)/shard_map/ppermute | solution.py:152
Sparse Core Ops, SparseCore 0:
  10.4 73.0 all-gather.3
  104.8 67.4 all-gather.5

commit v7 on v4

--- a/solution.py
+++ b/solution.py
@@ -58,7 +58,14 @@
     piece_blocks = piece_rows.shape[1] // BLOCK
     grouped = piece_rows.reshape(head_count, piece_blocks, BLOCK, pair_width)
     pick_ids = jnp.concatenate([wanted, glob_ids.astype(jnp.int32)])
-    picked = jnp.take(grouped, jnp.clip(pick_ids, 0, piece_blocks - 1), axis=1)
+    pick_at = jnp.clip(pick_ids, 0, piece_blocks - 1)
+    picked = jnp.concatenate(
+        [
+            lax.dynamic_slice_in_dim(grouped, pick_at[index], 1, axis=1)
+            for index in range(pick_ids.shape[0])
+        ],
+        axis=1,
+    )
     random_pairs = picked[:, : block_count * rand_count].reshape(
         head_count, block_count, rand_count, BLOCK, pair_width
     )

time: 184 us -> 202 us (1.098); the launches traced: 184 us -> 199 us
  waiting for transfers between devices: 129 us -> 78.9 us
  between operations: 14.5 us -> 63.7 us
  local copies, waits for them, and re-layouts: 13.5 us -> 29.7 us
    all_gather x1, waiting for transfers between devices: 69.1 us -> 19.3 us  [local(): piece_rows = lax.all_gather(paired, 'seq', axis=1, tiled=True)]
    unnamed x29 -> x50, local copies, waits for them, and re-layouts: 6.7 us -> 24.2 us
    gather x1 -> x0, local copies, waits for them, and re-layouts: 3.38 us -> none  [local(): picked = jnp.take(grouped, jnp.clip(pick_ids, 0, piece_blocks - 1), axis=1)]
where the time goes in v7:
time: 202 us; the launch traced here: 199 us
  waiting for transfers between devices  78.9 us (39%)
  between operations  63.7 us (32%)
  local copies, waits for them, and re-layouts  29.7 us (15%)
  starting transfers between devices  11.5 us (6%)
  matrix products  7.84 us (4%)
  other arithmetic  7.74 us (4%)
    ppermute x1, waiting for transfers between devices, local(): lax.ppermute(edge_out[:, BLOCK:], 'seq', rightward).astype(jnp.float32)  41.9 us
    unnamed x50, local copies, waits for them, and re-layouts  24.2 us
    all_gather x1, waiting for transfers between devices, local(): piece_rows = lax.all_gather(paired, 'seq', axis=1, tiled=True)  19.3 us
    all_gather x1, waiting for transfers between devices, local(): global_parts = lax.all_gather(global_terms, 'seq', axis=0)  12.5 us
    all_to_all x1, starting transfers between devices, local(): lax.all_to_all(outgoing_grads, 'seq', split_axis=1, concat_axis=1, tiled=...  5.84 us
    ppermute x1, waiting for transfers between devices, local(): lax.ppermute(edge_out[:, :BLOCK], 'seq', leftward).astype(jnp.float32)  5.14 us
  transfers between devices with their start and end apart: 5, of which 4 were waited for; matrix products, arithmetic and copies ran while one was open for 6% of the time, Pallas kernels for 0%

profile of v7, /device:TPU:1, one launch (start us, length us, event | category | flops | bytes accessed | tf_op | source)
XLA Modules:
  0.0 199.4 jit_solution(7931879303422635809)
XLA Ops:
  7.2 1.0 constant_dynamic-update-slice_fusion.1
  8.2 0.9 constant_dynamic-update-slice_fusion
  9.9 0.8 copy.54
  10.9 0.8 copy.52
  64.2 19.3 %all-gather.4.cloned.1.call-done = bf16[1,12288,256]{2,1,0:T(8,128)(2,1)} async-done(((bf16[1,512,256]{2,1,0:T(8,128)(2,1)}), bf16[1,12288,256]{2,1,0:T(8,128)(2,1)}) %all-gather.4.cloned.1.call-update) | async-done | bytes 6291472 | tf_op jit(solution)/shard_map/all_gather | solution.py:28
  83.5 0.8 constant_dynamic-slice_fusion.4
  84.3 1.0 pad_maximum_fusion.2
  85.3 0.8 constant_dynamic-update-slice_fusion.25
  102.8 0.8 constant_dynamic-slice_fusion.1
  105.8 1.0 fusion.13
  106.9 0.9 fusion
  109.4 1.5 copy.77
  110.9 5.8 %all-to-all-start = ((bf16[1,24,2,64,256]{4,3,2,0,1:T(8,128)(2,1)}), bf16[1,24,2,64,256]{4,3,2,0,1:T(8,128)(2,1)S(1)}, u32[]{:S(2)}, u32[]{:S(2)}) async-start(bf16[1,24,2,64,256]{4,3,2,0,1:T(8,128)(2,1)} %bitcast.73), calls=%async_computation | async-start | bytes 3145728 | tf_op jit(solution)/shard_map/all_to_all | solution.py:131
  117.0 1.2 fusion.6
  119.9 1.2 fusion.4
  121.4 3.7 %collective-permute-start = (bf16[1,64,256]{2,1,0:T(8,128)(2,1)S(1)}, bf16[1,64,256]{2,1,0:T(8,128)(2,1)S(1)}, u32[]{:S(2)}, u32[]{:S(2)}) collective-permute-start(bf16[1,64,256]{2,1,0:T(8,128)(2,1)S(1)} %get-tuple-element.40), channel_id=1, source_target_pairs={{0,32},{32,64},{64,96},{96,128},{128,160},{160,192},{192,224},{224... | collective-permute-start | bytes 98312 | tf_op jit(solution)/shard_map/ppermute | solution.py:144
  125.1 1.1 fusion.12
  126.3 1.9 collective-permute-start.1
  128.2 41.9 %collective-permute-done = bf16[1,64,256]{2,1,0:T(8,128)(2,1)S(1)} collective-permute-done((bf16[1,64,256]{2,1,0:T(8,128)(2,1)S(1)}, bf16[1,64,256]{2,1,0:T(8,128)(2,1)S(1)}, u32[]{:S(2)}, u32[]{:S(2)}) %collective-permute-start) | collective-permute-done | bytes 32800 | tf_op jit(solution)/shard_map/ppermute | solution.py:144
  170.1 5.1 %collective-permute-done.1 = bf16[1,64,256]{2,1,0:T(8,128)(2,1)S(1)} collective-permute-done((bf16[1,64,256]{2,1,0:T(8,128)(2,1)S(1)}, bf16[1,64,256]{2,1,0:T(8,128)(2,1)S(1)}, u32[]{:S(2)}, u32[]{:S(2)}) %collective-permute-start.1) | collective-permute-done | bytes 32800 | tf_op jit(solution)/shard_map/ppermute | solution.py:145
  175.3 12.5 %all-gather.6.cloned.1.call-done = bf16[48,64,256]{2,1,0:T(8,128)(2,1)} async-done(((bf16[2,64,256]{2,1,0:T(8,128)(2,1)}), bf16[48,64,256]{2,1,0:T(8,128)(2,1)}) %all-gather.6.cloned.1.call-update) | async-done | bytes 1572880 | tf_op jit(solution)/shard_map/all_gather | solution.py:147
  187.8 1.7 convert_reduce_fusion
  189.5 0.9 copy.78
  191.8 0.8 fusion.40
  (94 shorter events, 28.3 us)
Async XLA Ops:
  7.2 96.6 %copy-start = (bf16[1,512,128]{2,1,0:T(8,128)(2,1)S(1)}, bf16[1,512,128]{2,1,0:T(8,128)(2,1)}, u32[]{:S(2)}) copy-start(bf16[1,512,128]{2,1,0:T(8,128)(2,1)} %param.11) | copy-start | bytes 393220
  7.2 76.3 %all-gather.4.cloned.1.call-start = ((), (), s32[]{:S(2)}) async-start(), calls=%async_computation.1 | async-start | bytes 6553600 | tf_op jit(solution)/shard_map/all_gather | solution.py:28
  9.1 0.7 copy-start.1
  103.8 3.1 %copy-start.5 = (bf16[1,8,8,64,256]{4,3,2,1,0:T(8,128)(2,1)}, bf16[1,8,8,64,256]{4,3,2,1,0:T(8,128)(2,1)S(1)}, u32[]{:S(2)}) copy-start(bf16[1,8,8,64,256]{4,3,2,1,0:T(8,128)(2,1)S(1)} %broadcast_dynamic-update-slice_fusion) | copy-start | bytes 6291460
  104.9 0.9 copy-start.2
  107.8 1.1 copy-start.3
  110.9 78.6 %all-to-all-start = ((bf16[1,24,2,64,256]{4,3,2,0,1:T(8,128)(2,1)}), bf16[1,24,2,64,256]{4,3,2,0,1:T(8,128)(2,1)S(1)}, u32[]{:S(2)}, u32[]{:S(2)}) async-start(bf16[1,24,2,64,256]{4,3,2,0,1:T(8,128)(2,1)} %bitcast.73), calls=%async_computation | async-start | bytes 3145728 | tf_op jit(solution)/shard_map/all_to_all | solution.py:131
  116.7 2.9 %copy-start.7 = (s32[2]{0:T(128)S(1)}, s32[2]{0:T(128)}, u32[]{:S(2)}) copy-start(s32[2]{0:T(128)} %param.17) | copy-start | bytes 28
  116.7 71.1 %all-gather.6.cloned.1.call-start = ((), (), s32[]{:S(2)}) async-start(), calls=%async_computation.2 | async-start | bytes 1638400 | tf_op jit(solution)/shard_map/all_gather | solution.py:147
  121.1 4.0 %copy-start.6 = (bf16[1,8,8,64,256]{4,3,2,1,0:T(8,128)(2,1)S(1)}, bf16[1,8,8,64,256]{4,3,2,1,0:T(8,128)(2,1)}, u32[]{:S(2)}) copy-start(bf16[1,8,8,64,256]{4,3,2,1,0:T(8,128)(2,1)} %copy-done.5) | copy-start | bytes 6291460
  121.2 3.8 %copy-start.4 = (bf16[8,64,8,64]{1,3,2,0:T(8,128)(2,1)S(1)}, bf16[8,64,8,64]{1,3,2,0:T(8,128)(2,1)}, u32[]{:S(2)}) copy-start(bf16[8,64,8,64]{1,3,2,0:T(8,128)(2,1)} %copy-done.3) | copy-start | bytes 1572868
  121.4 48.7 %collective-permute-start = (bf16[1,64,256]{2,1,0:T(8,128)(2,1)S(1)}, bf16[1,64,256]{2,1,0:T(8,128)(2,1)S(1)}, u32[]{:S(2)}, u32[]{:S(2)}) collective-permute-start(bf16[1,64,256]{2,1,0:T(8,128)(2,1)S(1)} %get-tuple-element.40), channel_id=1, source_target_pairs={{0,32},{32,64},{64,96},{96,128},{128,160},{160,192},{192,224},{224... | collective-permute-start | bytes 98312 | tf_op jit(solution)/shard_map/ppermute | solution.py:144
  126.3 49.0 %collective-permute-start.1 = (bf16[1,64,256]{2,1,0:T(8,128)(2,1)S(1)}, bf16[1,64,256]{2,1,0:T(8,128)(2,1)S(1)}, u32[]{:S(2)}, u32[]{:S(2)}) collective-permute-start(bf16[1,64,256]{2,1,0:T(8,128)(2,1)S(1)} %get-tuple-element.39), channel_id=1, source_target_pairs={{32,0},{64,32},{96,64},{128,96},{160,128},{192,160},{224,192},{256... | collective-permute-start | bytes 98312 | tf_op jit(solution)/shard_map/ppermute | solution.py:145
Sparse Core Ops, SparseCore 0:
  10.4 73.0 all-gather.3
  120.6 67.1 all-gather.5

commit v8 on v6

--- a/solution.py
+++ b/solution.py
@@ -39,14 +39,15 @@
         ids = jnp.concatenate([owner_now * block_count + slot_now, glob_ids.astype(jnp.int32), edge_ids])
         return jnp.clip(ids, 0, total_blocks - 1)
 
-    def row_of(ids):
-        seq_of = ids // block_count
-        order_of = (seq_of % core_count) * (seq_count // core_count) + seq_of // core_count
-        return order_of * block_count + ids % block_count
-
     mine_ids = pick_list(seq_place)
-    all_rows = lax.all_gather(paired_blocks, ("sc", "sz"), axis=1, tiled=True)
-    picked = jnp.take(all_rows, row_of(mine_ids), axis=1)
+    sibling_blocks = lax.ppermute(paired_blocks, "sc", [(0, 1), (1, 0)])
+    chip_blocks = jnp.where(
+        core_place == 0,
+        jnp.concatenate([paired_blocks, sibling_blocks], axis=1),
+        jnp.concatenate([sibling_blocks, paired_blocks], axis=1),
+    )
+    all_rows = lax.all_gather(chip_blocks, "sz", axis=1, tiled=True)
+    picked = jnp.take(all_rows, mine_ids, axis=1)
     pick_count = block_count * rand_count + glob_count
     widened = jnp.concatenate(
         [picked[:, pick_count : pick_count + 1], paired_blocks, picked[:, pick_count + 1 :]], axis=1

time: 184 us -> 207 us (1.12)
  starting transfers between devices: 11.5 us -> 25.7 us
  waiting for transfers between devices: 128 us -> 141 us
  local copies, waits for them, and re-layouts: 13.4 us -> 10.6 us
    ppermute x0 -> x1, starting transfers between devices: none -> 12.4 us  [local(): sibling_blocks = lax.ppermute(paired_blocks, 'sc', [(0, 1), (1, 0)])]
    all_gather x1, waiting for transfers between devices: 68.4 us -> 80 us  [local(): all_rows = lax.all_gather(chip_blocks, 'sz', axis=1, tiled=True)]
    unnamed x27 -> x29, local copies, waits for them, and re-layouts: 7.35 us -> 4.62 us
  transfers between devices with their start and end apart: 5 -> 6, of which waited for: 4 -> 5; matrix products, arithmetic and copies ran while one was open for 7% -> 4% of each run, Pallas kernels for 0% -> 0%
where the time goes in v8:
time: 207 us
  waiting for transfers between devices  141 us (68%)
  starting transfers between devices  25.7 us (12%)
  between operations  14.6 us (7%)
  local copies, waits for them, and re-layouts  10.6 us (5%)
  matrix products  7.84 us (4%)
  other arithmetic  7.28 us (4%)
    all_gather x1, waiting for transfers between devices, local(): all_rows = lax.all_gather(chip_blocks, 'sz', axis=1, tiled=True)  80 us
    ppermute x1, waiting for transfers between devices, local(): lax.ppermute(edge_out[:, BLOCK:], SEQ, rightward).astype(jnp.float32)  42 us
    all_gather x1, waiting for transfers between devices, local(): global_parts = lax.all_gather(global_terms, SEQ, axis=0)  12.6 us
    ppermute x1, starting transfers between devices, local(): sibling_blocks = lax.ppermute(paired_blocks, 'sc', [(0, 1), (1, 0)])  12.4 us
    all_to_all x1, starting transfers between devices, local(): lax.all_to_all(outgoing_grads, SEQ, split_axis=1, concat_axis=1, tiled=True)  7.68 us
    ppermute x1, waiting for transfers between devices, local(): lax.ppermute(edge_out[:, :BLOCK], SEQ, leftward).astype(jnp.float32)  5.06 us
    unnamed x29, local copies, waits for them, and re-layouts  4.62 us
  transfers between devices with their start and end apart: 6, of which 5 were waited for; matrix products, arithmetic and copies ran while one was open for 4% of the time, Pallas kernels for 0%

profile of v8, /device:TPU:1, one launch (start us, length us, event | category | flops | bytes accessed | tf_op | source)
XLA Modules:
  0.0 206.8 jit_solution(7291309433898846501)
XLA Ops:
  7.3 1.0 constant_dynamic-update-slice_fusion.1
  8.2 0.9 constant_dynamic-update-slice_fusion
  9.2 12.4 %collective-permute-start = (bf16[1,8,64,256]{3,2,1,0:T(8,128)(2,1)S(1)}, bf16[1,8,64,256]{3,2,1,0:T(8,128)(2,1)S(1)}, u32[]{:S(2)}, u32[]{:S(2)}) collective-permute-start(bf16[1,8,64,256]{3,2,1,0:T(8,128)(2,1)S(1)} %bitcast.186), channel_id=1, source_target_pairs={{0,32},{32,0},{1,33},{33,1},{2,34},{34,2},{3,35},{35,3},{4,36},{36... | collective-permute-start | bytes 786440 | tf_op jit(solution)/shard_map/ppermute | solution.py:43
  21.6 1.1 collective-permute-done
  22.7 0.9 fusion.21
  24.4 0.7 fusion.46
  25.5 80.0 %all-gather.4.cloned.1.call-done = bf16[1,192,64,256]{3,2,0,1:T(8,128)(2,1)} async-done(((bf16[1,16,64,256]{3,2,0,1:T(8,128)(2,1)}), bf16[1,192,64,256]{3,2,0,1:T(8,128)(2,1)}) %all-gather.4.cloned.1.call-update) | async-done | bytes 6291472 | tf_op jit(solution)/shard_map/all_gather | solution.py:49
  105.5 3.4 %gather_fusion = bf16[28,64,256]{2,1,0:T(8,128)(2,1)S(1)} fusion(bf16[192,64,256]{2,1,0:T(8,128)(2,1)} %bitcast.204, s32[1024]{0:T(1024)S(1)} %pad_clamp_fusion), kind=kCustom, calls=%fused_computation | custom fusion | bytes 1835120 | tf_op jit(solution)/shard_map/jit(_take)/gather | solution.py:50
  111.4 1.0 fusion.13
  112.4 0.9 fusion
  114.9 1.5 copy.76
  116.5 7.7 %all-to-all-start = ((bf16[1,24,2,64,256]{4,3,2,0,1:T(8,128)(2,1)}), bf16[1,24,2,64,256]{4,3,2,0,1:T(8,128)(2,1)S(1)}, u32[]{:S(2)}, u32[]{:S(2)}) async-start(bf16[1,24,2,64,256]{4,3,2,0,1:T(8,128)(2,1)} %bitcast.51), calls=%async_computation | async-start | bytes 3145728 | tf_op jit(solution)/shard_map/all_to_all | solution.py:139
  124.4 1.2 fusion.6
  125.6 0.7 maximum_reduce_fusion
  127.3 1.2 fusion.4
  128.8 3.7 %collective-permute-start.1 = (bf16[1,64,256]{2,1,0:T(8,128)(2,1)S(1)}, bf16[1,64,256]{2,1,0:T(8,128)(2,1)S(1)}, u32[]{:S(2)}, u32[]{:S(2)}) collective-permute-start(bf16[1,64,256]{2,1,0:T(8,128)(2,1)S(1)} %get-tuple-element.37), channel_id=1, source_target_pairs={{0,32},{32,64},{64,96},{96,128},{128,160},{160,192},{192,224},{224... | collective-permute-start | bytes 98312 | tf_op jit(solution)/shard_map/ppermute | solution.py:152
  132.5 1.1 fusion.12
  133.6 1.9 collective-permute-start.2
  135.6 42.0 %collective-permute-done.1 = bf16[1,64,256]{2,1,0:T(8,128)(2,1)S(1)} collective-permute-done((bf16[1,64,256]{2,1,0:T(8,128)(2,1)S(1)}, bf16[1,64,256]{2,1,0:T(8,128)(2,1)S(1)}, u32[]{:S(2)}, u32[]{:S(2)}) %collective-permute-start.1) | collective-permute-done | bytes 32800 | tf_op jit(solution)/shard_map/ppermute | solution.py:152
  177.6 5.1 %collective-permute-done.2 = bf16[1,64,256]{2,1,0:T(8,128)(2,1)S(1)} collective-permute-done((bf16[1,64,256]{2,1,0:T(8,128)(2,1)S(1)}, bf16[1,64,256]{2,1,0:T(8,128)(2,1)S(1)}, u32[]{:S(2)}, u32[]{:S(2)}) %collective-permute-start.2) | collective-permute-done | bytes 32800 | tf_op jit(solution)/shard_map/ppermute | solution.py:153
  182.6 12.6 %all-gather.6.cloned.1.call-done = bf16[48,64,256]{2,1,0:T(8,128)(2,1)} async-done(((bf16[2,64,256]{2,1,0:T(8,128)(2,1)}), bf16[48,64,256]{2,1,0:T(8,128)(2,1)}) %all-gather.6.cloned.1.call-update) | async-done | bytes 1572880 | tf_op jit(solution)/shard_map/all_gather | solution.py:155
  195.3 1.7 convert_reduce_fusion
  196.9 0.9 copy.77
  199.2 0.8 fusion.45
  (80 shorter events, 8.0 us)
Async XLA Ops:
  7.2 102.2 %copy-start = (bf16[1,512,128]{2,1,0:T(8,128)(2,1)S(1)}, bf16[1,512,128]{2,1,0:T(8,128)(2,1)}, u32[]{:S(2)}) copy-start(bf16[1,512,128]{2,1,0:T(8,128)(2,1)} %param.12) | copy-start | bytes 393220
  7.2 18.1 %copy-start.9 = (s32[2]{0:T(128)S(1)}, s32[2]{0:T(128)}, u32[]{:S(2)}) copy-start(s32[2]{0:T(128)} %constant.129.clone) | copy-start | bytes 28
  7.2 16.5 %copy-start.6 = (s32[192,3]{0,1:T(4,128)S(1)}, s32[192,3]{0,1:T(4,128)}, u32[]{:S(2)}) copy-start(s32[192,3]{0,1:T(4,128)} %param.16) | copy-start | bytes 6916
  7.2 16.8 %copy-start.7 = (s32[192,3]{0,1:T(4,128)S(1)}, s32[192,3]{0,1:T(4,128)}, u32[]{:S(2)}) copy-start(s32[192,3]{0,1:T(4,128)} %param.17) | copy-start | bytes 6916
  7.2 18.1 %copy-start.8 = (s32[2]{0:T(128)S(1)}, s32[2]{0:T(128)}, u32[]{:S(2)}) copy-start(s32[2]{0:T(128)} %param.18) | copy-start | bytes 28
  7.2 98.3 %all-gather.4.cloned.1.call-start = ((), (), s32[]{:S(2)}) async-start(), calls=%async_computation.1 | async-start | bytes 6815744 | tf_op jit(solution)/shard_map/all_gather | solution.py:49
  9.2 13.5 %collective-permute-start = (bf16[1,8,64,256]{3,2,1,0:T(8,128)(2,1)S(1)}, bf16[1,8,64,256]{3,2,1,0:T(8,128)(2,1)S(1)}, u32[]{:S(2)}, u32[]{:S(2)}) collective-permute-start(bf16[1,8,64,256]{3,2,1,0:T(8,128)(2,1)S(1)} %bitcast.186), channel_id=1, source_target_pairs={{0,32},{32,0},{1,33},{33,1},{2,34},{34,2},{3,35},{35,3},{4,36},{36... | collective-permute-start | bytes 786440 | tf_op jit(solution)/shard_map/ppermute | solution.py:43
  109.3 3.1 %copy-start.4 = (bf16[1,8,8,64,256]{4,3,2,1,0:T(8,128)(2,1)}, bf16[1,8,8,64,256]{4,3,2,1,0:T(8,128)(2,1)S(1)}, u32[]{:S(2)}) copy-start(bf16[1,8,8,64,256]{4,3,2,1,0:T(8,128)(2,1)S(1)} %broadcast_dynamic-update-slice_fusion) | copy-start | bytes 6291460
  110.5 0.9 copy-start.1
  113.3 1.1 copy-start.2
  116.5 80.5 %all-to-all-start = ((bf16[1,24,2,64,256]{4,3,2,0,1:T(8,128)(2,1)}), bf16[1,24,2,64,256]{4,3,2,0,1:T(8,128)(2,1)S(1)}, u32[]{:S(2)}, u32[]{:S(2)}) async-start(bf16[1,24,2,64,256]{4,3,2,0,1:T(8,128)(2,1)} %bitcast.51), calls=%async_computation | async-start | bytes 3145728 | tf_op jit(solution)/shard_map/all_to_all | solution.py:139
  124.2 71.1 %all-gather.6.cloned.1.call-start = ((), (), s32[]{:S(2)}) async-start(), calls=%async_computation.2 | async-start | bytes 1638400 | tf_op jit(solution)/shard_map/all_gather | solution.py:155
  128.5 4.0 %copy-start.5 = (bf16[1,8,8,64,256]{4,3,2,1,0:T(8,128)(2,1)S(1)}, bf16[1,8,8,64,256]{4,3,2,1,0:T(8,128)(2,1)}, u32[]{:S(2)}) copy-start(bf16[1,8,8,64,256]{4,3,2,1,0:T(8,128)(2,1)} %copy-done.4) | copy-start | bytes 6291460
  128.6 3.9 %copy-start.3 = (bf16[8,64,8,64]{1,3,2,0:T(8,128)(2,1)S(1)}, bf16[8,64,8,64]{1,3,2,0:T(8,128)(2,1)}, u32[]{:S(2)}) copy-start(bf16[8,64,8,64]{1,3,2,0:T(8,128)(2,1)} %copy-done.2) | copy-start | bytes 1572868
  128.8 48.7 %collective-permute-start.1 = (bf16[1,64,256]{2,1,0:T(8,128)(2,1)S(1)}, bf16[1,64,256]{2,1,0:T(8,128)(2,1)S(1)}, u32[]{:S(2)}, u32[]{:S(2)}) collective-permute-start(bf16[1,64,256]{2,1,0:T(8,128)(2,1)S(1)} %get-tuple-element.37), channel_id=1, source_target_pairs={{0,32},{32,64},{64,96},{96,128},{128,160},{160,192},{192,224},{224... | collective-permute-start | bytes 98312 | tf_op jit(solution)/shard_map/ppermute | solution.py:152
  133.6 49.0 %collective-permute-start.2 = (bf16[1,64,256]{2,1,0:T(8,128)(2,1)S(1)}, bf16[1,64,256]{2,1,0:T(8,128)(2,1)S(1)}, u32[]{:S(2)}, u32[]{:S(2)}) collective-permute-start(bf16[1,64,256]{2,1,0:T(8,128)(2,1)S(1)} %get-tuple-element.36), channel_id=1, source_target_pairs={{32,0},{64,32},{96,64},{128,96},{160,128},{192,160},{224,192},{256... | collective-permute-start | bytes 98312 | tf_op jit(solution)/shard_map/ppermute | solution.py:153
Sparse Core Ops, SparseCore 0:
  23.8 81.6 all-gather.3
  128.0 67.2 all-gather.5

commit v9 on v4

--- a/solution.py
+++ b/solution.py
@@ -148,10 +148,10 @@
     gathered = jnp.einsum(
         "cb,ecx->ebx", block_hot.astype(jnp.bfloat16), returned, preferred_element_type=jnp.float32
     )
-    accum = accum + gathered.reshape(head_count, block_count, BLOCK, pair_width)
     global_sums = jnp.sum(global_parts.astype(jnp.float32), axis=0)
     at_first = (seq_place == 0).astype(jnp.float32)
-    accum = accum.at[:, glob_ids].add(global_sums * at_first)
+    accum = lax.optimization_barrier(accum.at[:, glob_ids].add(global_sums * at_first))
+    accum = accum + gathered.reshape(head_count, block_count, BLOCK, pair_width)
     grad_q = grad_query.reshape(head_count, row_count, head_width).astype(jnp.bfloat16)
     grad_k = accum[..., :head_width].reshape(head_count, row_count, head_width).astype(jnp.bfloat16)
     grad_v = accum[..., head_width:].reshape(head_count, row_count, head_width).astype(jnp.bfloat16)

time: 184 us -> 184 us (level)
    unnamed x29 -> x30, local copies, waits for them, and re-layouts: 6.7 us -> 6.73 us
  transfers between devices with their start and end apart: 5 -> 5, of which waited for: 4 -> 4; matrix products, arithmetic and copies ran while one was open for 6% -> 7% of each run, Pallas kernels for 0% -> 0%
where the time goes in v9:
time: 184 us
  waiting for transfers between devices  129 us (70%)
  between operations  14.5 us (8%)
  local copies, waits for them, and re-layouts  13.5 us (7%)
  starting transfers between devices  11.5 us (6%)
  matrix products  7.83 us (4%)
  other arithmetic  7.64 us (4%)
    all_gather x1, waiting for transfers between devices, local(): piece_rows = lax.all_gather(paired, 'seq', axis=1, tiled=True)  69.1 us
    ppermute x1, waiting for transfers between devices, local(): lax.ppermute(edge_out[:, BLOCK:], 'seq', rightward).astype(jnp.float32)  41.9 us
    all_gather x1, waiting for transfers between devices, local(): global_parts = lax.all_gather(global_terms, 'seq', axis=0)  12.7 us
    unnamed x30, local copies, waits for them, and re-layouts  6.73 us
    all_to_all x1, starting transfers between devices, local(): lax.all_to_all(outgoing_grads, 'seq', split_axis=1, concat_axis=1, tiled=...  5.83 us
    ppermute x1, waiting for transfers between devices, local(): lax.ppermute(edge_out[:, :BLOCK], 'seq', leftward).astype(jnp.float32)  5.02 us
  transfers between devices with their start and end apart: 5, of which 4 were waited for; matrix products, arithmetic and copies ran while one was open for 7% of the time, Pallas kernels for 0%

profile of v9, /device:TPU:1, one launch (start us, length us, event | category | flops | bytes accessed | tf_op | source)
XLA Modules:
  0.0 183.8 jit_solution(9458219556036639610)
XLA Ops:
  7.2 1.0 constant_dynamic-update-slice_fusion.1
  8.2 0.9 constant_dynamic-update-slice_fusion
  9.9 0.8 copy.52
  10.9 0.8 copy.54
  12.9 0.7 compare_and_fusion
  13.6 0.7 fusion.39
  14.4 69.1 %all-gather.4.cloned.1.call-done = bf16[1,12288,256]{2,1,0:T(8,128)(2,1)} async-done(((bf16[1,512,256]{2,1,0:T(8,128)(2,1)}), bf16[1,12288,256]{2,1,0:T(8,128)(2,1)}) %all-gather.4.cloned.1.call-update) | async-done | bytes 6291472 | tf_op jit(solution)/shard_map/all_gather | solution.py:28
  83.5 3.4 %gather_fusion = bf16[26,64,256]{2,1,0:T(8,128)(2,1)S(1)} fusion(bf16[192,64,256]{2,1,0:T(8,128)(2,1)} %bitcast.207, s32[1024]{0:T(1024)S(1)} %pad_clamp_fusion), kind=kCustom, calls=%fused_computation | custom fusion | bytes 1704040 | tf_op jit(solution)/shard_map/jit(_take)/gather | solution.py:61
  87.1 0.8 constant_dynamic-slice_fusion.2
  90.2 1.0 fusion.13
  91.2 0.9 fusion
  93.7 1.5 copy.77
  95.3 5.8 %all-to-all-start = ((bf16[1,24,2,64,256]{4,3,2,0,1:T(8,128)(2,1)}), bf16[1,24,2,64,256]{4,3,2,0,1:T(8,128)(2,1)S(1)}, u32[]{:S(2)}, u32[]{:S(2)}) async-start(bf16[1,24,2,64,256]{4,3,2,0,1:T(8,128)(2,1)} %bitcast.58), calls=%async_computation | async-start | bytes 3145728 | tf_op jit(solution)/shard_map/all_to_all | solution.py:124
  101.4 1.2 fusion.6
  104.2 1.2 fusion.4
  105.8 3.7 %collective-permute-start = (bf16[1,64,256]{2,1,0:T(8,128)(2,1)S(1)}, bf16[1,64,256]{2,1,0:T(8,128)(2,1)S(1)}, u32[]{:S(2)}, u32[]{:S(2)}) collective-permute-start(bf16[1,64,256]{2,1,0:T(8,128)(2,1)S(1)} %get-tuple-element.37), channel_id=1, source_target_pairs={{0,32},{32,64},{64,96},{96,128},{128,160},{160,192},{192,224},{224... | collective-permute-start | bytes 98312 | tf_op jit(solution)/shard_map/ppermute | solution.py:137
  109.5 1.1 fusion.12
  110.6 1.9 %collective-permute-start.1 = (bf16[1,64,256]{2,1,0:T(8,128)(2,1)S(1)}, bf16[1,64,256]{2,1,0:T(8,128)(2,1)S(1)}, u32[]{:S(2)}, u32[]{:S(2)}) collective-permute-start(bf16[1,64,256]{2,1,0:T(8,128)(2,1)S(1)} %get-tuple-element.36), channel_id=1, source_target_pairs={{32,0},{64,32},{96,64},{128,96},{160,128},{192,160},{224,192},{256... | collective-permute-start | bytes 98312 | tf_op jit(solution)/shard_map/ppermute | solution.py:138
  112.6 41.9 %collective-permute-done = bf16[1,64,256]{2,1,0:T(8,128)(2,1)S(1)} collective-permute-done((bf16[1,64,256]{2,1,0:T(8,128)(2,1)S(1)}, bf16[1,64,256]{2,1,0:T(8,128)(2,1)S(1)}, u32[]{:S(2)}, u32[]{:S(2)}) %collective-permute-start) | collective-permute-done | bytes 32800 | tf_op jit(solution)/shard_map/ppermute | solution.py:137
  154.6 5.0 %collective-permute-done.1 = bf16[1,64,256]{2,1,0:T(8,128)(2,1)S(1)} collective-permute-done((bf16[1,64,256]{2,1,0:T(8,128)(2,1)S(1)}, bf16[1,64,256]{2,1,0:T(8,128)(2,1)S(1)}, u32[]{:S(2)}, u32[]{:S(2)}) %collective-permute-start.1) | collective-permute-done | bytes 32800 | tf_op jit(solution)/shard_map/ppermute | solution.py:138
  159.6 12.7 %all-gather.6.cloned.1.call-done = bf16[48,64,256]{2,1,0:T(8,128)(2,1)} async-done(((bf16[2,64,256]{2,1,0:T(8,128)(2,1)}), bf16[48,64,256]{2,1,0:T(8,128)(2,1)}) %all-gather.6.cloned.1.call-update) | async-done | bytes 1572880 | tf_op jit(solution)/shard_map/all_gather | solution.py:140
  172.3 1.7 convert_reduce_fusion
  174.6 0.9 copy.78
  176.2 0.8 fusion.42
  (75 shorter events, 9.7 us)
Async XLA Ops:
  7.2 81.0 %copy-start = (bf16[1,512,128]{2,1,0:T(8,128)(2,1)S(1)}, bf16[1,512,128]{2,1,0:T(8,128)(2,1)}, u32[]{:S(2)}) copy-start(bf16[1,512,128]{2,1,0:T(8,128)(2,1)} %param.11) | copy-start | bytes 393220
  7.2 76.3 %all-gather.4.cloned.1.call-start = ((), (), s32[]{:S(2)}) async-start(), calls=%async_computation.1 | async-start | bytes 6553600 | tf_op jit(solution)/shard_map/all_gather | solution.py:28
  9.1 0.7 copy-start.1
  86.9 1.0 copy-start.2
  88.1 3.1 %copy-start.6 = (bf16[1,8,8,64,256]{4,3,2,1,0:T(8,128)(2,1)}, bf16[1,8,8,64,256]{4,3,2,1,0:T(8,128)(2,1)S(1)}, u32[]{:S(2)}) copy-start(bf16[1,8,8,64,256]{4,3,2,1,0:T(8,128)(2,1)S(1)} %broadcast_dynamic-update-slice_fusion) | copy-start | bytes 6291460
  89.3 0.9 copy-start.3
  92.1 1.0 copy-start.4
  95.3 79.4 %all-to-all-start = ((bf16[1,24,2,64,256]{4,3,2,0,1:T(8,128)(2,1)}), bf16[1,24,2,64,256]{4,3,2,0,1:T(8,128)(2,1)S(1)}, u32[]{:S(2)}, u32[]{:S(2)}) async-start(bf16[1,24,2,64,256]{4,3,2,0,1:T(8,128)(2,1)} %bitcast.58), calls=%async_computation | async-start | bytes 3145728 | tf_op jit(solution)/shard_map/all_to_all | solution.py:124
  101.1 2.9 %copy-start.8 = (s32[2]{0:T(128)S(1)}, s32[2]{0:T(128)}, u32[]{:S(2)}) copy-start(s32[2]{0:T(128)} %param.17) | copy-start | bytes 28
  101.1 71.2 %all-gather.6.cloned.1.call-start = ((), (), s32[]{:S(2)}) async-start(), calls=%async_computation.2 | async-start | bytes 1638400 | tf_op jit(solution)/shard_map/all_gather | solution.py:140
  105.5 4.0 %copy-start.7 = (bf16[1,8,8,64,256]{4,3,2,1,0:T(8,128)(2,1)S(1)}, bf16[1,8,8,64,256]{4,3,2,1,0:T(8,128)(2,1)}, u32[]{:S(2)}) copy-start(bf16[1,8,8,64,256]{4,3,2,1,0:T(8,128)(2,1)} %copy-done.6) | copy-start | bytes 6291460
  105.6 3.9 %copy-start.5 = (bf16[8,64,8,64]{1,3,2,0:T(8,128)(2,1)S(1)}, bf16[8,64,8,64]{1,3,2,0:T(8,128)(2,1)}, u32[]{:S(2)}) copy-start(bf16[8,64,8,64]{1,3,2,0:T(8,128)(2,1)} %copy-done.4) | copy-start | bytes 1572868
  105.8 48.7 %collective-permute-start = (bf16[1,64,256]{2,1,0:T(8,128)(2,1)S(1)}, bf16[1,64,256]{2,1,0:T(8,128)(2,1)S(1)}, u32[]{:S(2)}, u32[]{:S(2)}) collective-permute-start(bf16[1,64,256]{2,1,0:T(8,128)(2,1)S(1)} %get-tuple-element.37), channel_id=1, source_target_pairs={{0,32},{32,64},{64,96},{96,128},{128,160},{160,192},{192,224},{224... | collective-permute-start | bytes 98312 | tf_op jit(solution)/shard_map/ppermute | solution.py:137
  110.6 49.0 %collective-permute-start.1 = (bf16[1,64,256]{2,1,0:T(8,128)(2,1)S(1)}, bf16[1,64,256]{2,1,0:T(8,128)(2,1)S(1)}, u32[]{:S(2)}, u32[]{:S(2)}) collective-permute-start(bf16[1,64,256]{2,1,0:T(8,128)(2,1)S(1)} %get-tuple-element.36), channel_id=1, source_target_pairs={{32,0},{64,32},{96,64},{128,96},{160,128},{192,160},{224,192},{256... | collective-permute-start | bytes 98312 | tf_op jit(solution)/shard_map/ppermute | solution.py:138
Sparse Core Ops, SparseCore 0:
  10.4 73.0 all-gather.3
  104.9 67.3 all-gather.5

commit v10 on v4

--- a/solution.py
+++ b/solution.py
@@ -23,7 +23,9 @@
     )
     pair_width = 2 * head_width
     score_scale = 1.0 / math.sqrt(head_width)
-    paired = jnp.concatenate([keys, values], axis=2)
+    paired = jnp.pad(keys, ((0, 0), (0, 0), (0, head_width))) + jnp.pad(
+        values, ((0, 0), (0, 0), (head_width, 0))
+    )
     paired_blocks = paired.reshape(head_count, block_count, BLOCK, pair_width)
     piece_rows = lax.all_gather(paired, "seq", axis=1, tiled=True)
     row_start = seq_place * row_count

time: 184 us -> 184 us (level)
  local copies, waits for them, and re-layouts: 13.5 us -> 10.9 us
    unnamed x29 -> x26, local copies, waits for them, and re-layouts: 6.7 us -> 5.04 us
where the time goes in v10:
time: 184 us
  waiting for transfers between devices  130 us (71%)
  between operations  14.5 us (8%)
  starting transfers between devices  11.5 us (6%)
  local copies, waits for them, and re-layouts  10.9 us (6%)
  other arithmetic  9.41 us (5%)
  matrix products  7.83 us (4%)
    all_gather x1, waiting for transfers between devices, local(): piece_rows = lax.all_gather(paired, 'seq', axis=1, tiled=True)  70 us
    ppermute x1, waiting for transfers between devices, local(): lax.ppermute(edge_out[:, BLOCK:], 'seq', rightward).astype(jnp.float32)  41.9 us
    all_gather x1, waiting for transfers between devices, local(): global_parts = lax.all_gather(global_terms, 'seq', axis=0)  12.7 us
    all_to_all x1, starting transfers between devices, local(): lax.all_to_all(outgoing_grads, 'seq', split_axis=1, concat_axis=1, tiled=...  5.83 us
    ppermute x1, waiting for transfers between devices, local(): lax.ppermute(edge_out[:, :BLOCK], 'seq', leftward).astype(jnp.float32)  5.05 us
    unnamed x26, local copies, waits for them, and re-layouts  5.04 us
  transfers between devices with their start and end apart: 5, of which 4 were waited for; matrix products, arithmetic and copies ran while one was open for 6% of the time, Pallas kernels for 0%

profile of v10, /device:TPU:1, one launch (start us, length us, event | category | flops | bytes accessed | tf_op | source)
XLA Modules:
  0.0 183.9 jit_solution(15609462406319383814)
XLA Ops:
  7.2 1.7 pad_add_fusion.1
  9.0 0.8 copy.52
  10.0 0.8 copy.54
  11.1 0.7 fusion.42
  12.0 0.7 compare_and_fusion
  12.8 0.7 fusion.38
  13.5 70.0 %all-gather.4.cloned.1.call-done = bf16[1,12288,256]{2,1,0:T(8,128)(2,1)} async-done(((bf16[1,512,256]{2,1,0:T(8,128)(2,1)}), bf16[1,12288,256]{2,1,0:T(8,128)(2,1)}) %all-gather.4.cloned.1.call-update) | async-done | bytes 6291472 | tf_op jit(solution)/shard_map/all_gather | solution.py:30
  83.5 3.4 %gather_fusion = bf16[26,64,256]{2,1,0:T(8,128)(2,1)S(1)} fusion(bf16[192,64,256]{2,1,0:T(8,128)(2,1)} %bitcast.203, s32[1024]{0:T(1024)S(1)} %pad_clamp_fusion), kind=kCustom, calls=%fused_computation | custom fusion | bytes 1704040 | tf_op jit(solution)/shard_map/jit(_take)/gather | solution.py:63
  87.1 0.8 constant_dynamic-slice_fusion.2
  90.2 1.0 fusion.13
  91.2 0.9 fusion
  93.7 1.5 copy.77
  95.3 5.8 %all-to-all-start = ((bf16[1,24,2,64,256]{4,3,2,0,1:T(8,128)(2,1)}), bf16[1,24,2,64,256]{4,3,2,0,1:T(8,128)(2,1)S(1)}, u32[]{:S(2)}, u32[]{:S(2)}) async-start(bf16[1,24,2,64,256]{4,3,2,0,1:T(8,128)(2,1)} %bitcast.50), calls=%async_computation | async-start | bytes 3145728 | tf_op jit(solution)/shard_map/all_to_all | solution.py:126
  101.4 1.2 fusion.6
  104.2 1.2 fusion.4
  105.8 3.7 %collective-permute-start = (bf16[1,64,256]{2,1,0:T(8,128)(2,1)S(1)}, bf16[1,64,256]{2,1,0:T(8,128)(2,1)S(1)}, u32[]{:S(2)}, u32[]{:S(2)}) collective-permute-start(bf16[1,64,256]{2,1,0:T(8,128)(2,1)S(1)} %get-tuple-element.37), channel_id=1, source_target_pairs={{0,32},{32,64},{64,96},{96,128},{128,160},{160,192},{192,224},{224... | collective-permute-start | bytes 98312 | tf_op jit(solution)/shard_map/ppermute | solution.py:139
  109.5 1.1 fusion.12
  110.6 1.9 %collective-permute-start.1 = (bf16[1,64,256]{2,1,0:T(8,128)(2,1)S(1)}, bf16[1,64,256]{2,1,0:T(8,128)(2,1)S(1)}, u32[]{:S(2)}, u32[]{:S(2)}) collective-permute-start(bf16[1,64,256]{2,1,0:T(8,128)(2,1)S(1)} %get-tuple-element.36), channel_id=1, source_target_pairs={{32,0},{64,32},{96,64},{128,96},{160,128},{192,160},{224,192},{256... | collective-permute-start | bytes 98312 | tf_op jit(solution)/shard_map/ppermute | solution.py:140
  112.6 41.9 %collective-permute-done = bf16[1,64,256]{2,1,0:T(8,128)(2,1)S(1)} collective-permute-done((bf16[1,64,256]{2,1,0:T(8,128)(2,1)S(1)}, bf16[1,64,256]{2,1,0:T(8,128)(2,1)S(1)}, u32[]{:S(2)}, u32[]{:S(2)}) %collective-permute-start) | collective-permute-done | bytes 32800 | tf_op jit(solution)/shard_map/ppermute | solution.py:139
  154.5 5.1 %collective-permute-done.1 = bf16[1,64,256]{2,1,0:T(8,128)(2,1)S(1)} collective-permute-done((bf16[1,64,256]{2,1,0:T(8,128)(2,1)S(1)}, bf16[1,64,256]{2,1,0:T(8,128)(2,1)S(1)}, u32[]{:S(2)}, u32[]{:S(2)}) %collective-permute-start.1) | collective-permute-done | bytes 32800 | tf_op jit(solution)/shard_map/ppermute | solution.py:140
  159.6 12.7 %all-gather.6.cloned.1.call-done = bf16[48,64,256]{2,1,0:T(8,128)(2,1)} async-done(((bf16[2,64,256]{2,1,0:T(8,128)(2,1)}), bf16[48,64,256]{2,1,0:T(8,128)(2,1)}) %all-gather.6.cloned.1.call-update) | async-done | bytes 1572880 | tf_op jit(solution)/shard_map/all_gather | solution.py:142
  172.3 1.7 convert_reduce_fusion
  174.0 0.9 copy.78
  176.3 0.8 fusion.41
  (72 shorter events, 8.2 us)
Async XLA Ops:
  7.2 81.0 %copy-start = (bf16[1,512,128]{2,1,0:T(8,128)(2,1)S(1)}, bf16[1,512,128]{2,1,0:T(8,128)(2,1)}, u32[]{:S(2)}) copy-start(bf16[1,512,128]{2,1,0:T(8,128)(2,1)} %param.11) | copy-start | bytes 393220
  7.2 76.3 %all-gather.4.cloned.1.call-start = ((), (), s32[]{:S(2)}) async-start(), calls=%async_computation.1 | async-start | bytes 6553600 | tf_op jit(solution)/shard_map/all_gather | solution.py:30
  86.9 1.0 copy-start.1
  88.1 3.1 %copy-start.5 = (bf16[1,8,8,64,256]{4,3,2,1,0:T(8,128)(2,1)}, bf16[1,8,8,64,256]{4,3,2,1,0:T(8,128)(2,1)S(1)}, u32[]{:S(2)}) copy-start(bf16[1,8,8,64,256]{4,3,2,1,0:T(8,128)(2,1)S(1)} %broadcast_dynamic-update-slice_fusion) | copy-start | bytes 6291460
  89.3 0.9 copy-start.2
  92.1 1.0 copy-start.3
  95.3 78.7 %all-to-all-start = ((bf16[1,24,2,64,256]{4,3,2,0,1:T(8,128)(2,1)}), bf16[1,24,2,64,256]{4,3,2,0,1:T(8,128)(2,1)S(1)}, u32[]{:S(2)}, u32[]{:S(2)}) async-start(bf16[1,24,2,64,256]{4,3,2,0,1:T(8,128)(2,1)} %bitcast.50), calls=%async_computation | async-start | bytes 3145728 | tf_op jit(solution)/shard_map/all_to_all | solution.py:126
  101.1 2.9 %copy-start.7 = (s32[2]{0:T(128)S(1)}, s32[2]{0:T(128)}, u32[]{:S(2)}) copy-start(s32[2]{0:T(128)} %param.17) | copy-start | bytes 28
  101.1 71.2 %all-gather.6.cloned.1.call-start = ((), (), s32[]{:S(2)}) async-start(), calls=%async_computation.2 | async-start | bytes 1638400 | tf_op jit(solution)/shard_map/all_gather | solution.py:142
  105.5 4.0 %copy-start.6 = (bf16[1,8,8,64,256]{4,3,2,1,0:T(8,128)(2,1)S(1)}, bf16[1,8,8,64,256]{4,3,2,1,0:T(8,128)(2,1)}, u32[]{:S(2)}) copy-start(bf16[1,8,8,64,256]{4,3,2,1,0:T(8,128)(2,1)} %copy-done.5) | copy-start | bytes 6291460
  105.6 3.9 %copy-start.4 = (bf16[8,64,8,64]{1,3,2,0:T(8,128)(2,1)S(1)}, bf16[8,64,8,64]{1,3,2,0:T(8,128)(2,1)}, u32[]{:S(2)}) copy-start(bf16[8,64,8,64]{1,3,2,0:T(8,128)(2,1)} %copy-done.3) | copy-start | bytes 1572868
  105.8 48.7 %collective-permute-start = (bf16[1,64,256]{2,1,0:T(8,128)(2,1)S(1)}, bf16[1,64,256]{2,1,0:T(8,128)(2,1)S(1)}, u32[]{:S(2)}, u32[]{:S(2)}) collective-permute-start(bf16[1,64,256]{2,1,0:T(8,128)(2,1)S(1)} %get-tuple-element.37), channel_id=1, source_target_pairs={{0,32},{32,64},{64,96},{96,128},{128,160},{160,192},{192,224},{224... | collective-permute-start | bytes 98312 | tf_op jit(solution)/shard_map/ppermute | solution.py:139
  110.6 49.0 %collective-permute-start.1 = (bf16[1,64,256]{2,1,0:T(8,128)(2,1)S(1)}, bf16[1,64,256]{2,1,0:T(8,128)(2,1)S(1)}, u32[]{:S(2)}, u32[]{:S(2)}) collective-permute-start(bf16[1,64,256]{2,1,0:T(8,128)(2,1)S(1)} %get-tuple-element.36), channel_id=1, source_target_pairs={{32,0},{64,32},{96,64},{128,96},{160,128},{192,160},{224,192},{256... | collective-permute-start | bytes 98312 | tf_op jit(solution)/shard_map/ppermute | solution.py:140
Sparse Core Ops, SparseCore 0:
  10.4 73.0 all-gather.3
  104.9 67.3 all-gather.5
